TPU v7x, 128 devices: a whole 4x4x4 slice. The times are simulated.
128 devices in a mesh: gx: 4 (over z), gy: 32 (over y, x, core).
Axes of the slice: x: 4, y: 4, z: 4, core: 2. Of those that a mesh axis runs over, the one named last changes fastest.
Arguments:
- tokens: bfloat16 [32768, 1664], P('gy', 'gx'), may hold values from -6 to 6
- segment_ids: int32 [32768], P('gy'), may hold values from 0 to 1023, as said below
- first_gain: float32 [1664], replicated, may hold values from 0.5 to 2
- first_bias: float32 [1664], replicated, may hold values from -3 to 3
- query_key_value: bfloat16 [3, 1664, 1664], P(None, 'gy', 'gx'), may hold values from -0.15625 to 0.15625
- project_out: bfloat16 [1664, 1664], P('gx', 'gy'), may hold values from -0.15625 to 0.15625
- second_gain: float32 [1664], replicated, may hold values from 0.5 to 2
- second_bias: float32 [1664], replicated, may hold values from -3 to 3
- up_weight: bfloat16 [1664, 8192], P('gy', 'gx'), may hold values from -0.15625 to 0.15625
- down_weight: bfloat16 [8192, 1664], P('gx', 'gy'), may hold values from -0.0625 to 0.0625
- final_gain: float32 [1664], replicated, may hold values from 0.5 to 2
- final_bias: float32 [1664], replicated, may hold values from -3 to 3
- merge_weight: bfloat16 [4, 1664, 1664], P(None, 'gx', 'gy'), may hold values from -0.078125 to 0.078125
- owners: int32 [8192, 1], P('gy'), may hold values from 0 to 31; in each aligned block of 256 rows (0 to 255, 256 to 511, ...) at most 16 rows name the same one
Outputs:
- delivered: bfloat16 [32, 32, 16, 1664], P('gy', None, None, 'gx')
Inputs may be any that keep to these rules, and one draw needn't show every extreme that they name: `segment_ids`: each segment is a run of whole units of 32 consecutive tokens that lies inside one aligned block of 1024 tokens; ids never fall along the tokens and differ between segments. `owners`: in each aligned block of 256 rows (the merged tokens of one index of gy), no owner is named by more than 16 rows.
All inputs are finite; a program needn't handle non-finite values.
Results may differ from a plain program's by a relative error of at most 0.02.
Values may be sent and summed in bfloat16 or wider, within the bound.
No kernel may reach another device: no remote copies, remote signals or barrier semaphores. Data moves between devices by JAX's collectives and lax.ppermute only.
A program may use at most 128 MiB of HBM per device.

v0:
```python
import jax
import jax.numpy as jnp
from jax import lax
from jax.sharding import PartitionSpec as P

HEAD = 104
IMG_W = 16


EPSILON = 1e-06


def normalize_rows(values, gain, bias):
    values = values.astype(jnp.float32)
    center = values - jnp.mean(values, axis=-1, keepdims=True)
    spread = jnp.mean(center * center, axis=-1, keepdims=True)
    return center * lax.rsqrt(spread + EPSILON) * gain + bias


def normalize_from_sums(values, sums, features, gain, bias):
    values = values.astype(jnp.float32)
    row_mean = sums[0] / features
    spread = sums[1] / features - row_mean * row_mean
    return (values - row_mean[:, None]) * lax.rsqrt(spread[:, None] + EPSILON) * gain + bias


def own_slice(vector, width):
    return lax.dynamic_slice_in_dim(vector, lax.axis_index("gx") * width, width, 0)


def row_sums(values):
    values = values.astype(jnp.float32)
    return (jnp.sum(values, axis=-1), jnp.sum(values * values, axis=-1))


def ring_perm(n, shift):
    return [(j, (j + shift) % n) for j in range(n)]


def gx_gather_blocks(x, n):
    me = lax.axis_index("gx")
    half = x.shape[0] // 2
    from_left = lax.ppermute(x, "gx", ring_perm(n, 1))
    from_right = lax.ppermute(x, "gx", ring_perm(n, -1))
    far_top = lax.ppermute(from_left[:half], "gx", ring_perm(n, 1))
    far_bottom = lax.ppermute(from_right[half:], "gx", ring_perm(n, -1))
    far = jnp.concatenate([far_top, far_bottom], axis=0)
    relative = [x, from_right, far, from_left]
    doubled = jnp.stack(relative + relative, axis=1)
    return lax.dynamic_slice_in_dim(doubled, (n - me) % n, n, axis=1)


def gx_all_gather(x, n):
    blocks = gx_gather_blocks(x, n)
    return blocks.reshape(x.shape[0], n * x.shape[1])


def gx_matmul_reduce_scatter(lhs, w_blocks, contract, n):
    me = lax.axis_index("gx")
    half = lhs.shape[0] // 2
    top = lhs[:half]
    bottom = lhs[half:]

    def block(index):
        return lax.dynamic_index_in_dim(w_blocks, index % n, 0, keepdims=False)

    acc_top = contract(top, block(me - 1))
    acc_bottom = contract(bottom, block(me + 1))
    for step in range(1, n):
        got_top = lax.ppermute(acc_top.astype(jnp.bfloat16), "gx", ring_perm(n, 1))
        got_bottom = lax.ppermute(acc_bottom.astype(jnp.bfloat16), "gx", ring_perm(n, -1))
        acc_top = got_top.astype(jnp.float32) + contract(top, block(me - step - 1))
        acc_bottom = got_bottom.astype(jnp.float32) + contract(bottom, block(me + step + 1))
    return jnp.concatenate([acc_top, acc_bottom], axis=0)


def plain_dot(lhs, rhs):
    return jnp.dot(lhs, rhs, preferred_element_type=jnp.float32)


def merge_dot(lhs, rhs):
    return jnp.einsum("pkf,kfc->pc", lhs, rhs, preferred_element_type=jnp.float32)


def gx_sum_rows(sums, n):
    me = lax.axis_index("gx")
    relative = [sums] + [lax.ppermute(sums, "gx", ring_perm(n, -shift)) for shift in range(1, n)]
    doubled = jnp.stack(relative + relative, axis=1)
    blocks = lax.dynamic_slice_in_dim(doubled, (n - me) % n, n, axis=1)
    total = blocks[:, 0]
    for j in range(1, n):
        total = total + blocks[:, j]
    return total


def local_attention(qkv, segment_ids):
    tok_rows = qkv.shape[1]
    head_count = qkv.shape[2] // HEAD
    queries = qkv[0].reshape(tok_rows, head_count, HEAD)
    key_rows = qkv[1].reshape(tok_rows, head_count, HEAD)
    value_rows = qkv[2].reshape(tok_rows, head_count, HEAD)
    query_block = min(512, tok_rows)

    def one_block(index):
        first_query = index * query_block
        query_part = lax.dynamic_slice_in_dim(queries, first_query, query_block, 0)
        query_ids = lax.dynamic_slice_in_dim(segment_ids, first_query, query_block, 0)
        scores = jnp.einsum(
            "qhe,khe->hqk", query_part, key_rows, preferred_element_type=jnp.float32
        ) * HEAD ** (-0.5)
        same_segment = query_ids[None, :, None] == segment_ids[None, None, :]
        scores = jnp.where(same_segment, scores, -1e30)
        highest = jnp.max(scores, axis=-1, keepdims=True)
        raised = jnp.exp(scores - highest)
        shares = (raised / jnp.sum(raised, axis=-1, keepdims=True)).astype(jnp.bfloat16)
        return jnp.einsum(
            "hqk,khe->qhe", shares, value_rows, preferred_element_type=jnp.float32
        ).astype(jnp.bfloat16)

    blocks = lax.map(one_block, jnp.arange(tok_rows // query_block, dtype=jnp.int32))
    return blocks.reshape(tok_rows, head_count * HEAD)


def body(
    tokens,
    segment_ids,
    first_gain,
    first_bias,
    query_key_value,
    project_out,
    second_gain,
    second_bias,
    up_weight,
    down_weight,
    final_gain,
    final_bias,
    merge_weight,
    owners,
):
    tok_rows = tokens.shape[0]
    feature_cols = tokens.shape[1]
    n_gx = lax.axis_size("gx")
    features = feature_cols * n_gx
    qkv_all = lax.all_gather(query_key_value, "gy", axis=1, tiled=True)
    proj_all = lax.all_gather(project_out, "gy", axis=1, tiled=True)
    up_all = lax.all_gather(up_weight, "gy", axis=0, tiled=True)
    down_all = lax.all_gather(down_weight, "gy", axis=1, tiled=True)
    merge_all = lax.all_gather(merge_weight, "gy", axis=2, tiled=True)
    width = feature_cols
    proj_blocks = proj_all.reshape(proj_all.shape[0], n_gx, width).transpose(1, 0, 2)
    down_blocks = down_all.reshape(down_all.shape[0], n_gx, width).transpose(1, 0, 2)
    merge_blocks = merge_all.reshape(
        merge_all.shape[0], merge_all.shape[1], n_gx, width
    ).transpose(2, 0, 1, 3)
    full_rows = gx_all_gather(tokens, n_gx)
    normed = normalize_rows(full_rows, first_gain, first_bias).astype(jnp.bfloat16)
    columns = normed
    qkv = jnp.einsum(
        "td,kdc->ktc",
        columns,
        qkv_all,
        preferred_element_type=jnp.float32,
    ).astype(jnp.bfloat16)
    attended = local_attention(qkv, segment_ids)
    attn_share = gx_matmul_reduce_scatter(attended, proj_blocks, plain_dot, n_gx)
    first_resid = (tokens.astype(jnp.float32) + attn_share).astype(jnp.bfloat16)
    resid_rows = gx_all_gather(first_resid, n_gx)
    second_normed = normalize_rows(resid_rows, second_gain, second_bias).astype(jnp.bfloat16)
    columns = second_normed
    upper = jnp.dot(
        columns,
        up_all,
        preferred_element_type=jnp.float32,
    )
    hidden = jax.nn.gelu(upper, approximate=False).astype(jnp.bfloat16)
    mlp_share = gx_matmul_reduce_scatter(hidden, down_blocks, plain_dot, n_gx)
    second_resid = (first_resid.astype(jnp.float32) + mlp_share).astype(jnp.bfloat16)
    post_sums = gx_sum_rows(jnp.stack(row_sums(second_resid)), n_gx)
    final_normed = normalize_from_sums(
        second_resid,
        post_sums,
        features,
        own_slice(final_gain, feature_cols),
        own_slice(final_bias, feature_cols),
    ).astype(jnp.bfloat16)
    merged_rows = tok_rows // 4
    grouped = (
        final_normed.reshape(tok_rows // (2 * IMG_W), 2, IMG_W // 2, 2, feature_cols)
        .transpose(0, 2, 1, 3, 4)
        .reshape(merged_rows, 4, feature_cols)
    )
    projected = gx_matmul_reduce_scatter(grouped, merge_blocks, merge_dot, n_gx).astype(
        jnp.bfloat16
    )
    owner_count = lax.axis_size("gy")
    capacity = max(2, 2 * merged_rows // owner_count)
    owner_col = owners[:, 0]
    one_hot = (owner_col[:, None] == jnp.arange(owner_count, dtype=jnp.int32)[None, :]).astype(
        jnp.int32
    )
    slot_rank = jnp.sum((jnp.cumsum(one_hot, axis=0) - 1) * one_hot, axis=1)
    target = jnp.where(slot_rank < capacity, owner_col * capacity + slot_rank, -1)
    picks = (
        target[None, :] == jnp.arange(owner_count * capacity, dtype=jnp.int32)[:, None]
    ).astype(jnp.bfloat16)
    outgoing = jnp.dot(picks, projected, preferred_element_type=jnp.float32).astype(
        jnp.bfloat16
    ).reshape(owner_count, capacity, feature_cols)
    arrived = lax.all_to_all(outgoing, "gy", split_axis=0, concat_axis=0, tiled=True)
    return arrived.reshape(1, owner_count, capacity, feature_cols)


def solution(mesh):
    in_specs = (
        P("gy", "gx"),
        P("gy"),
        P(),
        P(),
        P(None, "gy", "gx"),
        P("gx", "gy"),
        P(),
        P(),
        P("gy", "gx"),
        P("gx", "gy"),
        P(),
        P(),
        P(None, "gx", "gy"),
        P("gy", None),
    )
    out_specs = P("gy", None, None, "gx")

    return jax.shard_map(body, mesh=mesh, in_specs=in_specs, out_specs=out_specs, check_vma=False)
```

profile of v0, /device:TPU:1, one launch (start us, length us, event | category | flops | bytes accessed | tf_op | source)
XLA Modules:
  0.0 397.5 jit_solution(4567070539656669137)
XLA Ops:
  7.3 1.7 copy.25
  10.4 2.5 collective-permute-start.1
  12.9 2.2 collective-permute-start
  15.3 18.6 %collective-permute-done.1 = bf16[1024,416]{0,1:T(8,128)(2,1)S(1)} collective-permute-done((bf16[1024,416]{0,1:T(8,128)(2,1)}, bf16[1024,416]{0,1:T(8,128)(2,1)S(1)}, u32[]{:S(2)}, u32[]{:S(2)}) %collective-permute-start.1) | collective-permute-done | bytes 852000 | tf_op jit(solution)/shard_map/ppermute | solution.py:43
  34.1 2.7 collective-permute-start.3
  36.8 1.2 bitcast_dynamic-update-slice_fusion.10
  38.1 7.3 %collective-permute-done.2 = bf16[512,416]{0,1:T(8,128)(2,1)S(1)} collective-permute-done((bf16[512,416]{0,1:T(8,128)(2,1)S(1)}, bf16[512,416]{0,1:T(8,128)(2,1)S(1)}, u32[]{:S(2)}, u32[]{:S(2)}) %collective-permute-start.2) | collective-permute-done | bytes 426016 | tf_op jit(solution)/shard_map/ppermute | solution.py:45
  46.5 3.6 dynamic-slice_convert_fusion
  51.0 7.9 %copy.24 = f32[1024,1664]{1,0:T(8,128)} copy(f32[1024,1664]{0,1:T(8,128)} %bitcast.269) | data formatting | bytes 13631488 | tf_op jit(solution)/shard_map/convert_element_type | solution.py:14
  58.9 2.7 reshape.226
  61.6 46.0 %all-gather.9.cloned.1.call-done = bf16[3,1664,416]{2,0,1:T(4,128)(2,1)} async-done(((bf16[3,52,416]{2,0,1:T(4,128)(2,1)}), bf16[3,1664,416]{2,0,1:T(4,128)(2,1)}) %all-gather.9.cloned.1.call-update) | async-done | bytes 4153360 | tf_op jit(solution)/shard_map/all_gather | solution.py:144
  107.6 10.7 %convert_bitcast_fusion = bf16[3,1024,416]{1,2,0:T(8,128)(2,1)S(1)} fusion(bf16[3,1664,416]{2,0,1:T(4,128)(2,1)} %all-gather.9.cloned.1.call-done, f32[1024,1664]{1,0:T(8,128)} %copy.24, f32[1664]{0:T(1024)S(1)} %copy-done.12, f32[1664]{0:T(1024)S(1)} %copy-done.13, f32[1024]{0:T(1024)S(1)} %add_rsqrt_fusion.2, f32[1024]{0:T(1024)S(1)} %broadcast_multiply_fusion.1), kind=kOutput, calls=%fused_computation.61 | convolution fusion | flops 4262821888 | bytes 13546496 | tf_op jit(solution)/shard_map/td,kdc->ktc/dot_general | solution.py:158
  118.4 1.6 fusion.186
  120.0 30.7 %while.10 = (s32[]{:T(128)}, bf16[2,512,4,104]{1,3,2,0:T(8,128)(2,1)}, s32[2]{0:T(128)S(1)}, s32[1024]{0:T(1024)S(1)}, bf16[1024,4,104]{0,2,1:T(8,128)(2,1)}, /*...) while((s32[]{:T(128)}, ...), condition=%wide.region_8.9_spmd, body=%wide.region_5.8_spmd.sunk | while | flops 885736448 | bytes 20409008 | solution.py:120
  121.7 7.6 %fusion.218 = (f32[4,512]{1,0:T(4,128)S(1)}, f32[4,512,1024]{2,1,0:T(8,128)}) fusion(pred[512,1024]{1,0:T(8,128)(4,1)S(1)} %broadcast_compare_fusion.2, bf16[1024,4,104]{0,2,1:T(8,128)(2,1)} %get-tuple-element.155, bf16[1024,4,104]{0,2,1:T(8,128)(2,1)} %get-tuple-element.154, s32[]{:T(128)S(6)} %select_n.177), kind=kOutput, calls=%fused_computation.250.clone.1 | convolution fusion | flops 444597248 | bytes 10199044 | tf_op jit(solution)/shard_map/while/body/eval_jaxpr/sub | solution.py:114
  129.3 5.8 %fusion.219 = bf16[2,512,4,104]{1,3,2,0:T(8,128)(2,1)} fusion(bf16[2,512,4,104]{1,3,2,0:T(8,128)(2,1)} %get-tuple-element.140, s32[]{:T(128)} %get-tuple-element.139, bf16[1024,4,104]{0,2,1:T(8,128)(2,1)} %get-tuple-element.156, f32[4,512,1024]{2,1,0:T(8,128)} %get-tuple-element.126, f32[4,512]{1,0:T(4,128)S(1)} %get-tuple-element.127), kind=kOutput, calls=%fused_computation.11.clone.1 | convolution fusion | flops 440614912 | bytes 9675264 | tf_op jit(solution)/shard_map/while/body/eval_jaxpr/hqk,khe->qhe/dot_general | solution.py:116
  136.8 7.6 %fusion.218 = (f32[4,512]{1,0:T(4,128)S(1)}, f32[4,512,1024]{2,1,0:T(8,128)}) fusion(pred[512,1024]{1,0:T(8,128)(4,1)S(1)} %broadcast_compare_fusion.2, bf16[1024,4,104]{0,2,1:T(8,128)(2,1)} %get-tuple-element.155, bf16[1024,4,104]{0,2,1:T(8,128)(2,1)} %get-tuple-element.154, s32[]{:T(128)S(6)} %select_n.177), kind=kOutput, calls=%fused_computation.250.clone.1 | convolution fusion | flops 444597248 | bytes 10199044 | tf_op jit(solution)/shard_map/while/body/eval_jaxpr/sub | solution.py:114
  144.4 6.2 %fusion.219 = bf16[2,512,4,104]{1,3,2,0:T(8,128)(2,1)} fusion(bf16[2,512,4,104]{1,3,2,0:T(8,128)(2,1)} %get-tuple-element.140, s32[]{:T(128)} %get-tuple-element.139, bf16[1024,4,104]{0,2,1:T(8,128)(2,1)} %get-tuple-element.156, f32[4,512,1024]{2,1,0:T(8,128)} %get-tuple-element.126, f32[4,512]{1,0:T(4,128)S(1)} %get-tuple-element.127), kind=kOutput, calls=%fused_computation.11.clone.1 | convolution fusion | flops 440614912 | bytes 9675264 | tf_op jit(solution)/shard_map/while/body/eval_jaxpr/hqk,khe->qhe/dot_general | solution.py:116
  150.7 1.2 fusion.188
  152.3 1.7 collective-permute-start.4
  154.4 1.5 collective-permute-start.7
  156.7 8.6 %collective-permute-done.4 = bf16[512,416]{0,1:T(8,128)(2,1)S(1)} collective-permute-done((bf16[512,416]{0,1:T(8,128)(2,1)S(1)}, bf16[512,416]{0,1:T(8,128)(2,1)S(1)}, u32[]{:S(2)}, u32[]{:S(2)}) %collective-permute-start.4) | collective-permute-done | bytes 426016 | tf_op jit(solution)/shard_map/ppermute | solution.py:70
  166.1 2.7 collective-permute-start.8
  169.2 8.1 %collective-permute-done.5 = bf16[512,416]{0,1:T(8,128)(2,1)S(1)} collective-permute-done((bf16[512,416]{0,1:T(8,128)(2,1)S(1)}, bf16[512,416]{0,1:T(8,128)(2,1)S(1)}, u32[]{:S(2)}, u32[]{:S(2)}) %collective-permute-start.5) | collective-permute-done | bytes 426016 | tf_op jit(solution)/shard_map/ppermute | solution.py:70
  177.7 2.7 collective-permute-start.9
  180.8 7.5 %collective-permute-done.6 = bf16[512,416]{0,1:T(8,128)(2,1)S(1)} collective-permute-done((bf16[512,416]{0,1:T(8,128)(2,1)S(1)}, bf16[512,416]{0,1:T(8,128)(2,1)S(1)}, u32[]{:S(2)}, u32[]{:S(2)}) %collective-permute-start.6) | collective-permute-done | bytes 426016 | tf_op jit(solution)/shard_map/ppermute | solution.py:70
  188.5 1.3 bitcast_dynamic-update-slice_fusion.4
  189.9 2.7 collective-permute-start.10
  195.0 13.9 %collective-permute-done.11 = bf16[1024,416]{0,1:T(8,128)(2,1)S(1)} collective-permute-done((bf16[1024,416]{0,1:T(8,128)(2,1)S(1)}, bf16[1024,416]{0,1:T(8,128)(2,1)S(1)}, u32[]{:S(2)}, u32[]{:S(2)}) %collective-permute-start.11) | collective-permute-done | bytes 852000 | tf_op jit(solution)/shard_map/ppermute | solution.py:43
  209.1 2.7 collective-permute-start.13
  212.7 5.3 %collective-permute-done.12 = bf16[512,416]{0,1:T(8,128)(2,1)S(1)} collective-permute-done((bf16[512,416]{0,1:T(8,128)(2,1)S(1)}, bf16[512,416]{0,1:T(8,128)(2,1)S(1)}, u32[]{:S(2)}, u32[]{:S(2)}) %collective-permute-start.12) | collective-permute-done | bytes 426016 | tf_op jit(solution)/shard_map/ppermute | solution.py:45
  224.1 2.7 convert_reduce_fusion
  226.9 3.2 multiply_reduce_fusion
  230.1 2.9 fusion.37
  233.0 11.9 %constant_dynamic-slice_fusion.7 = (bf16[4,416,1,416]{1,0,3,2:T(4,128)(2,1)}, bf16[4,416,1,416]{1,0,3,2:T(4,128)(2,1)}, bf16[4,416,1,416]{1,0,3,2:T(4,128)(2,1)}...) fusion(bf16[4,416,4,416]{1,0,3,2:T(4,128)(2,1)} %bitcast.270, ...), kind=kLoop, calls=%fused_computation.224 | loop fusion | bytes 22151200 | tf_op jit(solution)/shard_map/dynamic-slice.16
  244.9 8.7 %reshape.228 = bf16[1664,2048]{1,0:T(8,128)(2,1)} reshape(bf16[32,52,2048]{2,1,0:T(8,128)(2,1)} %all-gather.15.cloned.1.call-done) | data formatting | bytes 13631488
  253.6 28.9 %fusion.26 = bf16[1024,2048]{1,0:T(8,128)(2,1)} fusion(bf16[1024,1664]{0,1:T(8,128)(2,1)} %fusion.37, bf16[1664,2048]{1,0:T(8,128)(2,1)} %reshape.228), kind=kOutput, calls=%fused_computation.24 | convolution fusion | flops 7115636736 | bytes 14417920 | tf_op jit(solution)/shard_map/dot_general | solution.py:170
  282.5 8.6 %reshape.230 = bf16[1664,2048]{1,0:T(8,128)(2,1)} reshape(bf16[32,52,2048]{2,1,0:T(8,128)(2,1)} %all-gather.17.cloned.1.call-done) | data formatting | bytes 13631488
  291.1 3.3 fusion.97
  294.4 4.0 fusion.102
  298.7 1.1 fusion.75
  299.8 2.7 collective-permute-start.17
  302.5 1.1 fusion.73
  303.6 3.3 collective-permute-done.14
  306.8 1.1 add_convert_fusion.4
  308.0 1.1 add_convert_fusion.2
  309.1 2.7 collective-permute-start.18
  311.8 1.1 fusion.67
  312.9 3.3 collective-permute-done.15
  317.3 3.2 collective-permute-start.19
  320.5 1.1 fusion.65
  321.6 5.1 %collective-permute-done.16 = bf16[512,416]{0,1:T(8,128)(2,1)S(1)} collective-permute-done((bf16[512,416]{0,1:T(8,128)(2,1)S(1)}, bf16[512,416]{0,1:T(8,128)(2,1)S(1)}, u32[]{:S(2)}, u32[]{:S(2)}) %collective-permute-start.16) | collective-permute-done | bytes 426016 | tf_op jit(solution)/shard_map/ppermute | solution.py:70
  326.8 1.1 collective-permute-done.19
  328.5 3.2 collective-permute-start.20
  332.8 2.9 collective-permute-done.21
  338.3 2.2 fusion.116
  340.9 2.2 fusion.109
  344.5 2.7 collective-permute-start.26
  350.0 2.7 collective-permute-start.27
  352.7 1.3 collective-permute-done.24
  354.5 3.1 collective-permute-start.28
  357.6 1.3 collective-permute-done.25
  358.9 1.5 collective-permute-done.28
  361.0 28.8 %all_to_all.5 = bf16[32,16,416]{2,1,0:T(8,128)(2,1)S(1)} all-to-all(bf16[32,16,416]{2,1,0:T(8,128)(2,1)S(1)} %bitcast.298), channel_id=1, replica_groups=mesh['gx'=4,'gy'=32] {'gy'}, dimensions={0} | all-to-all | bytes 851968 | tf_op jit(solution)/shard_map/all_to_all | solution.py:209
  (165 shorter events, 31.8 us)
Async XLA Ops:
  6.5 39.0 %copy-start.1 = (bf16[1024,416]{0,1:T(8,128)(2,1)S(1)}, bf16[1024,416]{0,1:T(8,128)(2,1)}, u32[]{:S(2)}) copy-start(bf16[1024,416]{0,1:T(8,128)(2,1)} %param.16) | copy-start | bytes 2555908
  6.5 52.4 %all-gather.13.cloned.1.call-start = ((), (), s32[]{:S(2)}) async-start(), calls=%async_computation.3 | async-start | bytes 1892352 | tf_op jit(solution)/shard_map/all_gather | solution.py:145
  7.3 100.4 %all-gather.9.cloned.1.call-start = ((), (), s32[]{:S(2)}) async-start(), calls=%async_computation.1 | async-start | bytes 7028736 | tf_op jit(solution)/shard_map/all_gather | solution.py:144
  9.0 224.0 %all-gather.11.cloned.1.call-start = ((), (), s32[]{:S(2)}) async-start(), calls=%async_computation.2 | async-start | bytes 7028736 | tf_op jit(solution)/shard_map/all_gather | solution.py:148
  9.8 235.2 %all-gather.15.cloned.1.call-start = ((), (), s32[]{:S(2)}) async-start(), calls=%async_computation.4 | async-start | bytes 7569408 | tf_op jit(solution)/shard_map/all_gather | solution.py:146
  10.4 272.2 %all-gather.17.cloned.1.call-start = ((), (), s32[]{:S(2)}) async-start(), calls=%async_computation.5 | async-start | bytes 7569408 | tf_op jit(solution)/shard_map/all_gather | solution.py:147
  10.4 23.5 %collective-permute-start.1 = (bf16[1024,416]{0,1:T(8,128)(2,1)}, bf16[1024,416]{0,1:T(8,128)(2,1)S(1)}, u32[]{:S(2)}, u32[]{:S(2)}) collective-permute-start(bf16[1024,416]{0,1:T(8,128)(2,1)} %param.16), channel_id=1, source_target_pairs={{0,32},{32,64},{64,96},{96,0},{1,33},{33,65},{65,97},{97,1},{2,34}... | collective-permute-start | bytes 2555912 | tf_op jit(solution)/shard_map/ppermute | solution.py:43
  12.9 21.1 %collective-permute-start = (bf16[1024,416]{0,1:T(8,128)(2,1)}, bf16[1024,416]{0,1:T(8,128)(2,1)S(1)}, u32[]{:S(2)}, u32[]{:S(2)}) collective-permute-start(bf16[1024,416]{0,1:T(8,128)(2,1)} %param.16), channel_id=1, source_target_pairs={{0,96},{32,0},{64,32},{96,64},{1,97},{33,1},{65,33},{97,65},{2,98}... | collective-permute-start | bytes 2555912 | tf_op jit(solution)/shard_map/ppermute | solution.py:44
  33.9 11.4 %collective-permute-start.2 = (bf16[512,416]{0,1:T(8,128)(2,1)S(1)}, bf16[512,416]{0,1:T(8,128)(2,1)S(1)}, u32[]{:S(2)}, u32[]{:S(2)}) collective-permute-start(bf16[512,416]{0,1:T(8,128)(2,1)S(1)} %slice.103), channel_id=1, source_target_pairs={{0,32},{32,64},{64,96},{96,0},{1,33},{33,65},{65,97},{97,1},{2,34}... | collective-permute-start | bytes 1277960 | tf_op jit(solution)/shard_map/ppermute | solution.py:45
  34.1 11.3 %collective-permute-start.3 = (bf16[512,416]{0,1:T(8,128)(2,1)S(1)}, bf16[512,416]{0,1:T(8,128)(2,1)S(1)}, u32[]{:S(2)}, u32[]{:S(2)}) collective-permute-start(bf16[512,416]{0,1:T(8,128)(2,1)S(1)} %slice.104), channel_id=1, source_target_pairs={{0,96},{32,0},{64,32},{96,64},{1,97},{33,1},{65,33},{97,65},{2,98}... | collective-permute-start | bytes 1277960 | tf_op jit(solution)/shard_map/ppermute | solution.py:46
  51.0 56.6 %copy-start.12 = (f32[1664]{0:T(1024)S(1)}, f32[1664]{0:T(1024)}, u32[]{:S(2)}) copy-start(f32[1664]{0:T(1024)} %param.19) | copy-start | bytes 19972
  51.0 56.6 %copy-start.13 = (f32[1664]{0:T(1024)S(1)}, f32[1664]{0:T(1024)}, u32[]{:S(2)}) copy-start(f32[1664]{0:T(1024)} %param.18) | copy-start | bytes 19972
  61.6 58.4 %copy-start.8 = (s32[1024]{0:T(1024)S(1)}, s32[1024]{0:T(1024)}, u32[]{:S(2)}) copy-start(s32[1024]{0:T(1024)} %param.17) | copy-start | bytes 12292
  152.3 12.9 %collective-permute-start.4 = (bf16[512,416]{0,1:T(8,128)(2,1)S(1)}, bf16[512,416]{0,1:T(8,128)(2,1)S(1)}, u32[]{:S(2)}, u32[]{:S(2)}) collective-permute-start(bf16[512,416]{0,1:T(8,128)(2,1)S(1)} %convolution_convert_fusion.2), channel_id=1, source_target_pairs={{0,32},{32,64},{64,96},{96,0},{1,33},{33,65},{65,97},{97,1},{2,34}... | collective-permute-start | bytes 1277960 | tf_op jit(solution)/shard_map/ppermute | solution.py:70
  154.4 11.3 %collective-permute-start.7 = (bf16[512,416]{0,1:T(8,128)(2,1)S(1)}, bf16[512,416]{0,1:T(8,128)(2,1)S(1)}, u32[]{:S(2)}, u32[]{:S(2)}) collective-permute-start(bf16[512,416]{0,1:T(8,128)(2,1)S(1)} %convolution_convert_fusion.1), channel_id=1, source_target_pairs={{0,96},{32,0},{64,32},{96,64},{1,97},{33,1},{65,33},{97,65},{2,98}... | collective-permute-start | bytes 1277960 | tf_op jit(solution)/shard_map/ppermute | solution.py:71
  165.6 11.7 %collective-permute-start.5 = (bf16[512,416]{0,1:T(8,128)(2,1)S(1)}, bf16[512,416]{0,1:T(8,128)(2,1)S(1)}, u32[]{:S(2)}, u32[]{:S(2)}) collective-permute-start(bf16[512,416]{0,1:T(8,128)(2,1)S(1)} %add_convert_fusion.8), channel_id=1, source_target_pairs={{0,32},{32,64},{64,96},{96,0},{1,33},{33,65},{65,97},{97,1},{2,34}... | collective-permute-start | bytes 1277960 | tf_op jit(solution)/shard_map/ppermute | solution.py:70
  166.1 11.4 %collective-permute-start.8 = (bf16[512,416]{0,1:T(8,128)(2,1)S(1)}, bf16[512,416]{0,1:T(8,128)(2,1)S(1)}, u32[]{:S(2)}, u32[]{:S(2)}) collective-permute-start(bf16[512,416]{0,1:T(8,128)(2,1)S(1)} %add_convert_fusion.6), channel_id=1, source_target_pairs={{0,96},{32,0},{64,32},{96,64},{1,97},{33,1},{65,33},{97,65},{2,98}... | collective-permute-start | bytes 1277960 | tf_op jit(solution)/shard_map/ppermute | solution.py:71
  169.2 24.9 %copy-start.9 = (s32[256,1]{0,1:T(1,128)S(1)}, s32[256,1]{0,1:T(1,128)}, u32[]{:S(2)}) copy-start(s32[256,1]{0,1:T(1,128)} %param.29) | copy-start | bytes 3076
  177.5 10.8 %collective-permute-start.6 = (bf16[512,416]{0,1:T(8,128)(2,1)S(1)}, bf16[512,416]{0,1:T(8,128)(2,1)S(1)}, u32[]{:S(2)}, u32[]{:S(2)}) collective-permute-start(bf16[512,416]{0,1:T(8,128)(2,1)S(1)} %add_convert_fusion.7), channel_id=1, source_target_pairs={{0,32},{32,64},{64,96},{96,0},{1,33},{33,65},{65,97},{97,1},{2,34}... | collective-permute-start | bytes 1277960 | tf_op jit(solution)/shard_map/ppermute | solution.py:70
  177.7 10.7 %collective-permute-start.9 = (bf16[512,416]{0,1:T(8,128)(2,1)S(1)}, bf16[512,416]{0,1:T(8,128)(2,1)S(1)}, u32[]{:S(2)}, u32[]{:S(2)}) collective-permute-start(bf16[512,416]{0,1:T(8,128)(2,1)S(1)} %add_convert_fusion.5), channel_id=1, source_target_pairs={{0,96},{32,0},{64,32},{96,64},{1,97},{33,1},{65,33},{97,65},{2,98}... | collective-permute-start | bytes 1277960 | tf_op jit(solution)/shard_map/ppermute | solution.py:71
  189.9 19.0 %collective-permute-start.11 = (bf16[1024,416]{0,1:T(8,128)(2,1)S(1)}, bf16[1024,416]{0,1:T(8,128)(2,1)S(1)}, u32[]{:S(2)}, u32[]{:S(2)}) collective-permute-start(bf16[1024,416]{0,1:T(8,128)(2,1)S(1)} %get-tuple-element.61), channel_id=1, source_target_pairs={{0,32},{32,64},{64,96},{96,0},{1,33},{33,65},{65,97},{97,1},{2,34}... | collective-permute-start | bytes 2555912 | tf_op jit(solution)/shard_map/ppermute | solution.py:43
  189.9 19.1 %collective-permute-start.10 = (bf16[1024,416]{0,1:T(8,128)(2,1)S(1)}, bf16[1024,416]{0,1:T(8,128)(2,1)S(1)}, u32[]{:S(2)}, u32[]{:S(2)}) collective-permute-start(bf16[1024,416]{0,1:T(8,128)(2,1)S(1)} %get-tuple-element.61), channel_id=1, source_target_pairs={{0,96},{32,0},{64,32},{96,64},{1,97},{33,1},{65,33},{97,65},{2,98}... | collective-permute-start | bytes 2555912 | tf_op jit(solution)/shard_map/ppermute | solution.py:44
  208.9 9.1 %collective-permute-start.12 = (bf16[512,416]{0,1:T(8,128)(2,1)S(1)}, bf16[512,416]{0,1:T(8,128)(2,1)S(1)}, u32[]{:S(2)}, u32[]{:S(2)}) collective-permute-start(bf16[512,416]{0,1:T(8,128)(2,1)S(1)} %slice.108), channel_id=1, source_target_pairs={{0,32},{32,64},{64,96},{96,0},{1,33},{33,65},{65,97},{97,1},{2,34}... | collective-permute-start | bytes 1277960 | tf_op jit(solution)/shard_map/ppermute | solution.py:45
  209.1 9.0 %collective-permute-start.13 = (bf16[512,416]{0,1:T(8,128)(2,1)S(1)}, bf16[512,416]{0,1:T(8,128)(2,1)S(1)}, u32[]{:S(2)}, u32[]{:S(2)}) collective-permute-start(bf16[512,416]{0,1:T(8,128)(2,1)S(1)} %slice.109), channel_id=1, source_target_pairs={{0,96},{32,0},{64,32},{96,64},{1,97},{33,1},{65,33},{97,65},{2,98}... | collective-permute-start | bytes 1277960 | tf_op jit(solution)/shard_map/ppermute | solution.py:46
  220.1 10.0 %copy-start.10 = (f32[1664]{0:T(1024)S(1)}, f32[1664]{0:T(1024)}, u32[]{:S(2)}) copy-start(f32[1664]{0:T(1024)} %param.23) | copy-start | bytes 19972
  220.1 10.0 %copy-start.11 = (f32[1664]{0:T(1024)S(1)}, f32[1664]{0:T(1024)}, u32[]{:S(2)}) copy-start(f32[1664]{0:T(1024)} %param.22) | copy-start | bytes 19972
  224.1 6.0 %copy-start = (bf16[1024,8,416]{0,2,1:T(8,128)(2,1)S(1)}, bf16[1024,8,416]{0,2,1:T(8,128)(2,1)}, u32[]{:S(2)}) copy-start(bf16[1024,8,416]{0,2,1:T(8,128)(2,1)} %bitcast_dynamic-update-slice_fusion.1) | copy-start | bytes 20447236
  291.1 7.6 %slice-start = ((s8[6815744]{0:T(1024)(128)(4,1)}), s8[4194304]{0:T(1024)(128)(4,1)S(1)}, s32[]{:S(2)}) async-start(s8[6815744]{0:T(1024)(128)(4,1)} %bitcast.289), calls=%async_computation.6 | async-start | bytes 8388608
  291.1 7.6 %copy-start.14 = (bf16[1024,2048]{1,0:T(8,128)(2,1)S(1)}, bf16[1024,2048]{1,0:T(8,128)(2,1)}, u32[]{:S(2)}) copy-start(bf16[1024,2048]{1,0:T(8,128)(2,1)} %fusion.26) | copy-start | bytes 12582916
  291.1 7.6 %slice-start.1 = ((s8[6815744]{0:T(1024)(128)(4,1)}), s8[2621440]{0:T(1024)(128)(4,1)S(1)}, s32[]{:S(2)}) async-start(s8[6815744]{0:T(1024)(128)(4,1)} %bitcast.289), calls=%async_computation.7 | async-start | bytes 5242880
  298.4 8.5 %collective-permute-start.14 = (bf16[512,416]{0,1:T(8,128)(2,1)S(1)}, bf16[512,416]{0,1:T(8,128)(2,1)S(1)}, u32[]{:S(2)}, u32[]{:S(2)}) collective-permute-start(bf16[512,416]{0,1:T(8,128)(2,1)S(1)} %fusion.97), channel_id=1, source_target_pairs={{0,32},{32,64},{64,96},{96,0},{1,33},{33,65},{65,97},{97,1},{2,34}... | collective-permute-start | bytes 1277960 | tf_op jit(solution)/shard_map/ppermute | solution.py:70
  299.8 8.2 %collective-permute-start.17 = (bf16[512,416]{0,1:T(8,128)(2,1)S(1)}, bf16[512,416]{0,1:T(8,128)(2,1)S(1)}, u32[]{:S(2)}, u32[]{:S(2)}) collective-permute-start(bf16[512,416]{0,1:T(8,128)(2,1)S(1)} %fusion.102), channel_id=1, source_target_pairs={{0,96},{32,0},{64,32},{96,64},{1,97},{33,1},{65,33},{97,65},{2,98}... | collective-permute-start | bytes 1277960 | tf_op jit(solution)/shard_map/ppermute | solution.py:71
  307.9 8.3 %collective-permute-start.15 = (bf16[512,416]{0,1:T(8,128)(2,1)S(1)}, bf16[512,416]{0,1:T(8,128)(2,1)S(1)}, u32[]{:S(2)}, u32[]{:S(2)}) collective-permute-start(bf16[512,416]{0,1:T(8,128)(2,1)S(1)} %add_convert_fusion.4), channel_id=1, source_target_pairs={{0,32},{32,64},{64,96},{96,0},{1,33},{33,65},{65,97},{97,1},{2,34}... | collective-permute-start | bytes 1277960 | tf_op jit(solution)/shard_map/ppermute | solution.py:70
  309.1 8.1 %collective-permute-start.18 = (bf16[512,416]{0,1:T(8,128)(2,1)S(1)}, bf16[512,416]{0,1:T(8,128)(2,1)S(1)}, u32[]{:S(2)}, u32[]{:S(2)}) collective-permute-start(bf16[512,416]{0,1:T(8,128)(2,1)S(1)} %add_convert_fusion.2), channel_id=1, source_target_pairs={{0,96},{32,0},{64,32},{96,64},{1,97},{33,1},{65,33},{97,65},{2,98}... | collective-permute-start | bytes 1277960 | tf_op jit(solution)/shard_map/ppermute | solution.py:71
  316.3 10.3 %collective-permute-start.16 = (bf16[512,416]{0,1:T(8,128)(2,1)S(1)}, bf16[512,416]{0,1:T(8,128)(2,1)S(1)}, u32[]{:S(2)}, u32[]{:S(2)}) collective-permute-start(bf16[512,416]{0,1:T(8,128)(2,1)S(1)} %add_convert_fusion.3), channel_id=1, source_target_pairs={{0,32},{32,64},{64,96},{96,0},{1,33},{33,65},{65,97},{97,1},{2,34}... | collective-permute-start | bytes 1277960 | tf_op jit(solution)/shard_map/ppermute | solution.py:70
  317.3 10.6 %collective-permute-start.19 = (bf16[512,416]{0,1:T(8,128)(2,1)S(1)}, bf16[512,416]{0,1:T(8,128)(2,1)S(1)}, u32[]{:S(2)}, u32[]{:S(2)}) collective-permute-start(bf16[512,416]{0,1:T(8,128)(2,1)S(1)} %add_convert_fusion.1), channel_id=1, source_target_pairs={{0,96},{32,0},{64,32},{96,64},{1,97},{33,1},{65,33},{97,65},{2,98}... | collective-permute-start | bytes 1277960 | tf_op jit(solution)/shard_map/ppermute | solution.py:71
  328.5 4.4 %collective-permute-start.20 = (f32[2,1024]{1,0:T(2,128)S(1)}, f32[2,1024]{1,0:T(2,128)S(1)}, u32[]{:S(2)}, u32[]{:S(2)}) collective-permute-start(f32[2,1024]{1,0:T(2,128)S(1)} %pad_maximum_fusion), channel_id=1, source_target_pairs={{0,96},{32,0},{64,32},{96,64},{1,97},{33,1},{65,33},{97,65},{2,98}... | collective-permute-start | bytes 24584 | tf_op jit(solution)/shard_map/ppermute | solution.py:87
  331.7 4.1 %collective-permute-start.21 = (f32[2,1024]{1,0:T(2,128)S(1)}, f32[2,1024]{1,0:T(2,128)S(1)}, u32[]{:S(2)}, u32[]{:S(2)}) collective-permute-start(f32[2,1024]{1,0:T(2,128)S(1)} %pad_maximum_fusion), channel_id=1, source_target_pairs={{0,64},{32,96},{64,0},{96,32},{1,65},{33,97},{65,1},{97,33},{2,66}... | collective-permute-start | bytes 24584 | tf_op jit(solution)/shard_map/ppermute | solution.py:87
  332.0 3.8 collective-permute-start.22
  337.3 5.8 %copy-start.7 = (bf16[4,416,1,416]{1,0,3,2:T(4,128)(2,1)S(1)}, bf16[4,416,1,416]{1,0,3,2:T(4,128)(2,1)}, u32[]{:S(2)}) copy-start(bf16[4,416,1,416]{1,0,3,2:T(4,128)(2,1)} %get-tuple-element.68) | copy-start | bytes 4153348
  337.3 6.5 %copy-start.6 = (bf16[4,416,1,416]{1,0,3,2:T(4,128)(2,1)S(1)}, bf16[4,416,1,416]{1,0,3,2:T(4,128)(2,1)}, u32[]{:S(2)}) copy-start(bf16[4,416,1,416]{1,0,3,2:T(4,128)(2,1)} %get-tuple-element.67) | copy-start | bytes 4153348
  338.2 8.9 %copy-start.5 = (bf16[4,416,1,416]{1,0,3,2:T(4,128)(2,1)S(1)}, bf16[4,416,1,416]{1,0,3,2:T(4,128)(2,1)}, u32[]{:S(2)}) copy-start(bf16[4,416,1,416]{1,0,3,2:T(4,128)(2,1)} %get-tuple-element.65) | copy-start | bytes 4153348
  338.3 9.5 %copy-start.4 = (bf16[4,416,1,416]{1,0,3,2:T(4,128)(2,1)S(1)}, bf16[4,416,1,416]{1,0,3,2:T(4,128)(2,1)}, u32[]{:S(2)}) copy-start(bf16[4,416,1,416]{1,0,3,2:T(4,128)(2,1)} %get-tuple-element.71) | copy-start | bytes 4153348
  340.6 7.9 %collective-permute-start.23 = (bf16[128,416]{0,1:T(8,128)(2,1)S(1)}, bf16[128,416]{0,1:T(8,128)(2,1)S(1)}, u32[]{:S(2)}, u32[]{:S(2)}) collective-permute-start(bf16[128,416]{0,1:T(8,128)(2,1)S(1)} %fusion.116), channel_id=1, source_target_pairs={{0,32},{32,64},{64,96},{96,0},{1,33},{33,65},{65,97},{97,1},{2,34}... | collective-permute-start | bytes 319496 | tf_op jit(solution)/shard_map/ppermute | solution.py:70
  340.9 7.6 %copy-start.3 = (bf16[4,416,1,416]{1,0,3,2:T(4,128)(2,1)S(1)}, bf16[4,416,1,416]{1,0,3,2:T(4,128)(2,1)}, u32[]{:S(2)}) copy-start(bf16[4,416,1,416]{1,0,3,2:T(4,128)(2,1)} %get-tuple-element.70) | copy-start | bytes 4153348
  343.1 6.2 %copy-start.2 = (bf16[4,416,1,416]{1,0,3,2:T(4,128)(2,1)S(1)}, bf16[4,416,1,416]{1,0,3,2:T(4,128)(2,1)}, u32[]{:S(2)}) copy-start(bf16[4,416,1,416]{1,0,3,2:T(4,128)(2,1)} %get-tuple-element.66) | copy-start | bytes 4153348
  344.5 4.8 %collective-permute-start.26 = (bf16[128,416]{0,1:T(8,128)(2,1)S(1)}, bf16[128,416]{0,1:T(8,128)(2,1)S(1)}, u32[]{:S(2)}, u32[]{:S(2)}) collective-permute-start(bf16[128,416]{0,1:T(8,128)(2,1)S(1)} %fusion.115), channel_id=1, source_target_pairs={{0,96},{32,0},{64,32},{96,64},{1,97},{33,1},{65,33},{97,65},{2,98}... | collective-permute-start | bytes 319496 | tf_op jit(solution)/shard_map/ppermute | solution.py:71
  349.2 4.8 %collective-permute-start.24 = (bf16[128,416]{0,1:T(8,128)(2,1)S(1)}, bf16[128,416]{0,1:T(8,128)(2,1)S(1)}, u32[]{:S(2)}, u32[]{:S(2)}) collective-permute-start(bf16[128,416]{0,1:T(8,128)(2,1)S(1)} %add_convert_fusion.14), channel_id=1, source_target_pairs={{0,32},{32,64},{64,96},{96,0},{1,33},{33,65},{65,97},{97,1},{2,34}... | collective-permute-start | bytes 319496 | tf_op jit(solution)/shard_map/ppermute | solution.py:70
  350.0 4.4 %collective-permute-start.27 = (bf16[128,416]{0,1:T(8,128)(2,1)S(1)}, bf16[128,416]{0,1:T(8,128)(2,1)S(1)}, u32[]{:S(2)}, u32[]{:S(2)}) collective-permute-start(bf16[128,416]{0,1:T(8,128)(2,1)S(1)} %add_convert_fusion.11), channel_id=1, source_target_pairs={{0,96},{32,0},{64,32},{96,64},{1,97},{33,1},{65,33},{97,65},{2,98}... | collective-permute-start | bytes 319496 | tf_op jit(solution)/shard_map/ppermute | solution.py:71
  354.1 4.8 %collective-permute-start.25 = (bf16[128,416]{0,1:T(8,128)(2,1)S(1)}, bf16[128,416]{0,1:T(8,128)(2,1)S(1)}, u32[]{:S(2)}, u32[]{:S(2)}) collective-permute-start(bf16[128,416]{0,1:T(8,128)(2,1)S(1)} %add_convert_fusion.13), channel_id=1, source_target_pairs={{0,32},{32,64},{64,96},{96,0},{1,33},{33,65},{65,97},{97,1},{2,34}... | collective-permute-start | bytes 319496 | tf_op jit(solution)/shard_map/ppermute | solution.py:70
  354.5 5.9 %collective-permute-start.28 = (bf16[128,416]{0,1:T(8,128)(2,1)S(1)}, bf16[128,416]{0,1:T(8,128)(2,1)S(1)}, u32[]{:S(2)}, u32[]{:S(2)}) collective-permute-start(bf16[128,416]{0,1:T(8,128)(2,1)S(1)} %add_convert_fusion.10), channel_id=1, source_target_pairs={{0,96},{32,0},{64,32},{96,64},{1,97},{33,1},{65,33},{97,65},{2,98}... | collective-permute-start | bytes 319496 | tf_op jit(solution)/shard_map/ppermute | solution.py:71
Sparse Core Ops, SparseCore 0:
  9.6 46.5 all-gather.12
  58.5 49.1 all-gather.8
  109.9 48.5 all-gather.10
  160.6 49.4 all-gather.14
  212.2 49.7 all-gather.16
where the time goes:
time: 402 us; the launch traced here: 398 us
  waiting for transfers between devices  138 us (34%)
  matrix products  92.3 us (23%)
  local copies, waits for them, and re-layouts  57.1 us (14%)
  starting transfers between devices  44.4 us (11%)
  blocking collectives  28.8 us (7%)
  other arithmetic  21 us (5%)
  between operations  14.5 us (4%)
    all_gather x1, waiting for transfers between devices, body(): qkv_all = lax.all_gather(query_key_value, 'gy', axis=1, tiled=True)  46 us
    ppermute x9, waiting for transfers between devices, gx_matmul_reduce_scatter(): got_top = lax.ppermute(acc_top.astype(jnp.bfloat16), 'gx', ring_perm(n, 1))  38.3 us
    ppermute x2, waiting for transfers between devices, gx_gather_blocks(): from_left = lax.ppermute(x, 'gx', ring_perm(n, 1))  32.5 us
    dot_general x1, matrix products, body(): upper = jnp.dot(columns, up_all, preferred_element_type=jnp.float32)  28.9 us
    all_to_all x1, blocking collectives, body(): lax.all_to_all(outgoing, 'gy', split_axis=0, concat_axis=0, tiled=True)  28.8 us
    unnamed x53, local copies, waits for them, and re-layouts  28 us
    ppermute x9, starting transfers between devices, gx_matmul_reduce_scatter(): lax.ppermute(acc_bottom.astype(jnp.bfloat16), 'gx', ring_perm(n, -1))  24.1 us
    dot_general x16, matrix products, plain_dot(): return jnp.dot(lhs, rhs, preferred_element_type=jnp.float32)  16.7 us
  transfers between devices with their start and end apart: 34, of which 18 were waited for; matrix products, arithmetic and copies ran while one was open for 37% of the time, Pallas kernels for 0%

commit v1 on v0

--- a/solution.py
+++ b/solution.py
@@ -37,7 +37,7 @@
     return [(j, (j + shift) % n) for j in range(n)]
 
 
-def gx_gather_blocks(x, n):
+def gx_all_gather(x, n):
     me = lax.axis_index("gx")
     half = x.shape[0] // 2
     from_left = lax.ppermute(x, "gx", ring_perm(n, 1))
@@ -46,13 +46,14 @@
     far_bottom = lax.ppermute(from_right[half:], "gx", ring_perm(n, -1))
     far = jnp.concatenate([far_top, far_bottom], axis=0)
     relative = [x, from_right, far, from_left]
-    doubled = jnp.stack(relative + relative, axis=1)
-    return lax.dynamic_slice_in_dim(doubled, (n - me) % n, n, axis=1)
-
-
-def gx_all_gather(x, n):
-    blocks = gx_gather_blocks(x, n)
-    return blocks.reshape(x.shape[0], n * x.shape[1])
+    columns = []
+    for j in range(n):
+        offset = (j - me) % n
+        block = relative[n - 1]
+        for k in range(n - 2, -1, -1):
+            block = jnp.where(offset == k, relative[k], block)
+        columns.append(block)
+    return jnp.concatenate(columns, axis=1)
 
 
 def gx_matmul_reduce_scatter(lhs, w_blocks, contract, n):

time: 402 us -> 390 us (0.970)
  local copies, waits for them, and re-layouts: 57.1 us -> 43.2 us
  other arithmetic: 21 us -> 10.8 us
  waiting for transfers between devices: 138 us -> 148 us
    convert_element_type x1 -> x0, local copies, waits for them, and re-layouts: 7.87 us -> none  [normalize_rows(): values = values.astype(jnp.float32)]
    all_gather x1, waiting for transfers between devices: 0.01 us -> 7.01 us  [body(): proj_all = lax.all_gather(project_out, 'gy', axis=1, tiled=True)]
    convert_element_type x2 -> x1, other arithmetic: 6.48 us -> 0.29 us  [body(): first_resid = (tokens.astype(jnp.float32) + attn_share).astype(jnp.bfloat16)]
    unnamed x53 -> x54, local copies, waits for them, and re-layouts: 28 us -> 23.1 us
    another operation x4 -> x2, local copies, waits for them, and re-layouts: 12.9 us -> 12 us
  transfers between devices with their start and end apart: 34 -> 34, of which waited for: 18 -> 19; matrix products, arithmetic and copies ran while one was open for 37% -> 32% of each run, Pallas kernels for 0% -> 0%
where the time goes in v1:
time: 390 us; the launch traced here: 387 us
  waiting for transfers between devices  148 us (38%)
  matrix products  93.7 us (24%)
  starting transfers between devices  44 us (11%)
  local copies, waits for them, and re-layouts  43.2 us (11%)
  blocking collectives  30.8 us (8%)
  between operations  14.5 us (4%)
  other arithmetic  10.8 us (3%)
    all_gather x1, waiting for transfers between devices, body(): qkv_all = lax.all_gather(query_key_value, 'gy', axis=1, tiled=True)  48.7 us
    ppermute x9, waiting for transfers between devices, gx_matmul_reduce_scatter(): got_top = lax.ppermute(acc_top.astype(jnp.bfloat16), 'gx', ring_perm(n, 1))  38.8 us
    ppermute x2, waiting for transfers between devices, gx_all_gather(): from_left = lax.ppermute(x, 'gx', ring_perm(n, 1))  33 us
    dot_general x1, matrix products, body(): upper = jnp.dot(columns, up_all, preferred_element_type=jnp.float32)  32.1 us
    all_to_all x1, blocking collectives, body(): lax.all_to_all(outgoing, 'gy', split_axis=0, concat_axis=0, tiled=True)  30.8 us
    ppermute x9, starting transfers between devices, gx_matmul_reduce_scatter(): lax.ppermute(acc_bottom.astype(jnp.bfloat16), 'gx', ring_perm(n, -1))  24.2 us
    unnamed x54, local copies, waits for them, and re-layouts  23.1 us
    dot_general x16, matrix products, plain_dot(): return jnp.dot(lhs, rhs, preferred_element_type=jnp.float32)  16.7 us
  transfers between devices with their start and end apart: 34, of which 19 were waited for; matrix products, arithmetic and copies ran while one was open for 32% of the time, Pallas kernels for 0%

profile of v1, /device:TPU:1, one launch (start us, length us, event | category | flops | bytes accessed | tf_op | source)
XLA Modules:
  0.0 386.9 jit_solution(12809118590722159499)
XLA Ops:
  7.3 1.7 copy.24
  10.4 2.5 collective-permute-start.1
  12.9 2.2 collective-permute-start
  15.1 18.8 %collective-permute-done.1 = bf16[1024,416]{0,1:T(8,128)(2,1)S(1)} collective-permute-done((bf16[1024,416]{0,1:T(8,128)(2,1)}, bf16[1024,416]{0,1:T(8,128)(2,1)S(1)}, u32[]{:S(2)}, u32[]{:S(2)}) %collective-permute-start.1) | collective-permute-done | bytes 852000 | tf_op jit(solution)/shard_map/ppermute | solution.py:43
  34.1 2.7 collective-permute-start.3
  37.0 8.3 %collective-permute-done.2 = bf16[512,416]{0,1:T(8,128)(2,1)S(1)} collective-permute-done((bf16[512,416]{0,1:T(8,128)(2,1)S(1)}, bf16[512,416]{0,1:T(8,128)(2,1)S(1)}, u32[]{:S(2)}, u32[]{:S(2)}) %collective-permute-start.2) | collective-permute-done | bytes 426016 | tf_op jit(solution)/shard_map/ppermute | solution.py:45
  45.4 1.6 select_select_fusion.7
  47.1 1.1 convert_reduce_fusion.1
  48.1 1.0 fusion.42
  49.2 7.0 %all-gather.13.cloned.1.call-done = bf16[32,52,416]{2,1,0:T(8,128)(2,1)} async-done(((bf16[1,52,416]{2,1,0:T(8,128)(2,1)}), bf16[32,52,416]{2,1,0:T(8,128)(2,1)}) %all-gather.13.cloned.1.call-update) | async-done | bytes 1384464 | tf_op jit(solution)/shard_map/all_gather | solution.py:146
  56.2 2.7 reshape.208
  58.9 48.7 %all-gather.9.cloned.1.call-done = bf16[3,1664,416]{2,0,1:T(4,128)(2,1)} async-done(((bf16[3,52,416]{2,0,1:T(4,128)(2,1)}), bf16[3,1664,416]{2,0,1:T(4,128)(2,1)}) %all-gather.9.cloned.1.call-update) | async-done | bytes 4153360 | tf_op jit(solution)/shard_map/all_gather | solution.py:145
  107.6 9.2 %convert_bitcast_fusion = bf16[3,1024,416]{1,2,0:T(8,128)(2,1)S(1)} fusion(bf16[3,1664,416]{2,0,1:T(4,128)(2,1)} %all-gather.9.cloned.1.call-done, f32[1664]{0:T(1024)S(1)} %copy-done.14, f32[1664]{0:T(1024)S(1)} %copy-done.15, f32[1024]{0:T(1024)S(1)} %add_rsqrt_fusion.2, f32[1024]{0:T(1024)S(1)} %broadcast_multiply_fusion.1, ...), kind=kOutput, calls=%fused_computation.73 | convolution fusion | flops 4276453376 | bytes 10138624 | tf_op jit(solution)/shard_map/td,kdc->ktc/dot_general | solution.py:159
  116.9 1.4 fusion.197
  118.3 30.5 %while.10 = (s32[]{:T(128)}, bf16[2,512,4,104]{1,3,2,0:T(8,128)(2,1)}, s32[2]{0:T(128)S(1)}, s32[1024]{0:T(1024)S(1)}, bf16[1024,4,104]{0,2,1:T(8,128)(2,1)}, /*...) while((s32[]{:T(128)}, ...), condition=%wide.region_8.9_spmd, body=%wide.region_5.8_spmd.sunk | while | flops 885736448 | bytes 20409008 | solution.py:121
  120.0 7.7 %fusion.228 = (f32[4,512]{1,0:T(4,128)S(1)}, f32[4,512,1024]{2,1,0:T(8,128)}) fusion(pred[512,1024]{1,0:T(8,128)(4,1)S(1)} %broadcast_compare_fusion.2, bf16[1024,4,104]{0,2,1:T(8,128)(2,1)} %get-tuple-element.161, bf16[1024,4,104]{0,2,1:T(8,128)(2,1)} %get-tuple-element.160, s32[]{:T(128)S(6)} %select_n.405), kind=kOutput, calls=%fused_computation.256.clone.1 | convolution fusion | flops 444597248 | bytes 10199044 | tf_op jit(solution)/shard_map/while/body/eval_jaxpr/sub | solution.py:115
  127.7 5.7 %fusion.229 = bf16[2,512,4,104]{1,3,2,0:T(8,128)(2,1)} fusion(bf16[2,512,4,104]{1,3,2,0:T(8,128)(2,1)} %get-tuple-element.146, s32[]{:T(128)} %get-tuple-element.145, bf16[1024,4,104]{0,2,1:T(8,128)(2,1)S(1)} %get-tuple-element.162, f32[4,512,1024]{2,1,0:T(8,128)} %get-tuple-element.132, f32[4,512]{1,0:T(4,128)S(1)} %get-tuple-element.133), kind=kOutput, calls=%fused_computation.11.clone.1 | convolution fusion | flops 440614912 | bytes 9675264 | tf_op jit(solution)/shard_map/while/body/eval_jaxpr/hqk,khe->qhe/dot_general | solution.py:117
  135.0 7.7 %fusion.228 = (f32[4,512]{1,0:T(4,128)S(1)}, f32[4,512,1024]{2,1,0:T(8,128)}) fusion(pred[512,1024]{1,0:T(8,128)(4,1)S(1)} %broadcast_compare_fusion.2, bf16[1024,4,104]{0,2,1:T(8,128)(2,1)} %get-tuple-element.161, bf16[1024,4,104]{0,2,1:T(8,128)(2,1)} %get-tuple-element.160, s32[]{:T(128)S(6)} %select_n.405), kind=kOutput, calls=%fused_computation.256.clone.1 | convolution fusion | flops 444597248 | bytes 10199044 | tf_op jit(solution)/shard_map/while/body/eval_jaxpr/sub | solution.py:115
  142.7 6.0 %fusion.229 = bf16[2,512,4,104]{1,3,2,0:T(8,128)(2,1)} fusion(bf16[2,512,4,104]{1,3,2,0:T(8,128)(2,1)} %get-tuple-element.146, s32[]{:T(128)} %get-tuple-element.145, bf16[1024,4,104]{0,2,1:T(8,128)(2,1)S(1)} %get-tuple-element.162, f32[4,512,1024]{2,1,0:T(8,128)} %get-tuple-element.132, f32[4,512]{1,0:T(4,128)S(1)} %get-tuple-element.133), kind=kOutput, calls=%fused_computation.11.clone.1 | convolution fusion | flops 440614912 | bytes 9675264 | tf_op jit(solution)/shard_map/while/body/eval_jaxpr/hqk,khe->qhe/dot_general | solution.py:117
  148.8 1.2 fusion.199
  150.4 1.3 collective-permute-start.4
  152.2 1.5 collective-permute-start.7
  154.4 8.5 %collective-permute-done.4 = bf16[512,416]{0,1:T(8,128)(2,1)S(1)} collective-permute-done((bf16[512,416]{0,1:T(8,128)(2,1)S(1)}, bf16[512,416]{0,1:T(8,128)(2,1)S(1)}, u32[]{:S(2)}, u32[]{:S(2)}) %collective-permute-start.4) | collective-permute-done | bytes 426016 | tf_op jit(solution)/shard_map/ppermute | solution.py:71
  163.8 2.7 collective-permute-start.8
  166.9 8.0 %collective-permute-done.5 = bf16[512,416]{0,1:T(8,128)(2,1)S(1)} collective-permute-done((bf16[512,416]{0,1:T(8,128)(2,1)S(1)}, bf16[512,416]{0,1:T(8,128)(2,1)S(1)}, u32[]{:S(2)}, u32[]{:S(2)}) %collective-permute-start.5) | collective-permute-done | bytes 426016 | tf_op jit(solution)/shard_map/ppermute | solution.py:71
  175.3 2.7 collective-permute-start.9
  178.4 7.4 %collective-permute-done.6 = bf16[512,416]{0,1:T(8,128)(2,1)S(1)} collective-permute-done((bf16[512,416]{0,1:T(8,128)(2,1)S(1)}, bf16[512,416]{0,1:T(8,128)(2,1)S(1)}, u32[]{:S(2)}, u32[]{:S(2)}) %collective-permute-start.6) | collective-permute-done | bytes 426016 | tf_op jit(solution)/shard_map/ppermute | solution.py:71
  186.5 2.7 collective-permute-start.10
  191.3 14.2 %collective-permute-done.11 = bf16[1024,416]{0,1:T(8,128)(2,1)S(1)} collective-permute-done((bf16[1024,416]{0,1:T(8,128)(2,1)S(1)}, bf16[1024,416]{0,1:T(8,128)(2,1)S(1)}, u32[]{:S(2)}, u32[]{:S(2)}) %collective-permute-start.11) | collective-permute-done | bytes 852000 | tf_op jit(solution)/shard_map/ppermute | solution.py:43
  205.9 2.7 collective-permute-start.13
  208.7 6.0 %collective-permute-done.12 = bf16[512,416]{0,1:T(8,128)(2,1)S(1)} collective-permute-done((bf16[512,416]{0,1:T(8,128)(2,1)S(1)}, bf16[512,416]{0,1:T(8,128)(2,1)S(1)}, u32[]{:S(2)}, u32[]{:S(2)}) %collective-permute-start.12) | collective-permute-done | bytes 426016 | tf_op jit(solution)/shard_map/ppermute | solution.py:45
  214.8 1.8 select_select_fusion.3
  217.6 1.0 fusion.38
  218.6 12.0 %constant_dynamic-slice_fusion.7 = (bf16[4,416,1,416]{1,0,3,2:T(4,128)(2,1)}, bf16[4,416,1,416]{1,0,3,2:T(4,128)(2,1)}, bf16[4,416,1,416]{1,0,3,2:T(4,128)(2,1)}...) fusion(bf16[4,416,4,416]{1,0,3,2:T(4,128)(2,1)} %bitcast.227, ...), kind=kLoop, calls=%fused_computation.230 | loop fusion | bytes 22151200 | tf_op jit(solution)/shard_map/dynamic-slice.16
  230.6 8.8 %reshape.210 = bf16[1664,2048]{1,0:T(8,128)(2,1)} reshape(bf16[32,52,2048]{2,1,0:T(8,128)(2,1)} %all-gather.15.cloned.1.call-done) | data formatting | bytes 13631488
  239.4 32.1 %fusion.26 = bf16[1024,2048]{1,0:T(8,128)(2,1)} fusion(bf16[1664,2048]{1,0:T(8,128)(2,1)} %reshape.210, f32[1664]{0:T(1024)S(1)} %copy-done.16, f32[1664]{0:T(1024)S(1)} %copy-done.17, f32[1024]{0:T(1024)S(1)} %add_rsqrt_fusion.1, f32[1024]{0:T(1024)S(1)} %broadcast_multiply_fusion, bf16[1024,416]{0,1:T(8,128)(2,1)S(1)} %get-tuple-element.71, ...), kind=kOutput, calls=%fused_computation.28 | convolution fusion | flops 7137787904 | bytes 14439424 | tf_op jit(solution)/shard_map/dot_general | solution.py:171
  271.5 8.6 %reshape.212 = bf16[1664,2048]{1,0:T(8,128)(2,1)} reshape(bf16[32,52,2048]{2,1,0:T(8,128)(2,1)} %all-gather.17.cloned.1.call-done) | data formatting | bytes 13631488
  280.2 3.3 fusion.113
  283.5 4.0 %fusion.118 = bf16[512,416]{0,1:T(8,128)(2,1)S(1)} fusion(bf16[2048,4,416]{0,2,1:T(8,128)(2,1)} %bitcast.245, s32[]{:T(128)S(6)} %select_n.321, bf16[1024,2048]{1,0:T(8,128)(2,1)} %fusion.26), kind=kOutput, calls=%fused_computation.132 | convolution fusion | flops 872628224 | bytes 4227076 | tf_op jit(solution)/shard_map/dot_general | solution.py:79
  287.6 1.1 fusion.91
  288.7 2.7 collective-permute-start.17
  291.4 1.1 fusion.89
  292.4 3.8 collective-permute-done.14
  296.2 1.1 add_convert_fusion.3
  297.4 1.1 add_convert_fusion.1
  298.5 2.7 collective-permute-start.18
  301.2 1.1 fusion.83
  302.3 3.3 collective-permute-done.15
  306.4 3.4 collective-permute-start.19
  309.8 1.1 fusion.81
  310.9 4.4 %collective-permute-done.16 = bf16[512,416]{0,1:T(8,128)(2,1)S(1)} collective-permute-done((bf16[512,416]{0,1:T(8,128)(2,1)S(1)}, bf16[512,416]{0,1:T(8,128)(2,1)S(1)}, u32[]{:S(2)}, u32[]{:S(2)}) %collective-permute-start.16) | collective-permute-done | bytes 426016 | tf_op jit(solution)/shard_map/ppermute | solution.py:71
  315.5 0.9 collective-permute-done.19
  316.9 3.2 collective-permute-start.20
  320.7 0.8 collective-permute-start.22
  321.5 2.6 collective-permute-done.21
  325.9 0.9 fusion.198
  326.9 2.2 fusion.132
  329.2 2.2 fusion.125
  332.8 2.7 collective-permute-start.26
  338.3 2.7 collective-permute-start.27
  341.1 1.7 collective-permute-done.24
  342.9 3.0 collective-permute-start.28
  345.9 1.7 collective-permute-done.25
  348.5 30.8 %all_to_all.5 = bf16[32,16,416]{2,1,0:T(8,128)(2,1)S(1)} all-to-all(bf16[32,16,416]{2,1,0:T(8,128)(2,1)S(1)} %bitcast.255), channel_id=1, replica_groups=mesh['gx'=4,'gy'=32] {'gy'}, dimensions={0} | all-to-all | bytes 851968 | tf_op jit(solution)/shard_map/all_to_all | solution.py:210
  (161 shorter events, 22.1 us)
Async XLA Ops:
  6.5 49.7 %all-gather.13.cloned.1.call-start = ((), (), s32[]{:S(2)}) async-start(), calls=%async_computation.3 | async-start | bytes 1892352 | tf_op jit(solution)/shard_map/all_gather | solution.py:146
  7.3 100.4 %all-gather.9.cloned.1.call-start = ((), (), s32[]{:S(2)}) async-start(), calls=%async_computation.1 | async-start | bytes 7028736 | tf_op jit(solution)/shard_map/all_gather | solution.py:145
  9.0 209.6 %all-gather.11.cloned.1.call-start = ((), (), s32[]{:S(2)}) async-start(), calls=%async_computation.2 | async-start | bytes 7028736 | tf_op jit(solution)/shard_map/all_gather | solution.py:149
  9.8 220.9 %all-gather.15.cloned.1.call-start = ((), (), s32[]{:S(2)}) async-start(), calls=%async_computation.4 | async-start | bytes 7569408 | tf_op jit(solution)/shard_map/all_gather | solution.py:147
  10.4 261.2 %all-gather.17.cloned.1.call-start = ((), (), s32[]{:S(2)}) async-start(), calls=%async_computation.5 | async-start | bytes 7569408 | tf_op jit(solution)/shard_map/all_gather | solution.py:148
  10.4 23.5 %collective-permute-start.1 = (bf16[1024,416]{0,1:T(8,128)(2,1)}, bf16[1024,416]{0,1:T(8,128)(2,1)S(1)}, u32[]{:S(2)}, u32[]{:S(2)}) collective-permute-start(bf16[1024,416]{0,1:T(8,128)(2,1)} %param.16), channel_id=1, source_target_pairs={{0,32},{32,64},{64,96},{96,0},{1,33},{33,65},{65,97},{97,1},{2,34}... | collective-permute-start | bytes 2555912 | tf_op jit(solution)/shard_map/ppermute | solution.py:43
  12.9 21.1 %collective-permute-start = (bf16[1024,416]{0,1:T(8,128)(2,1)}, bf16[1024,416]{0,1:T(8,128)(2,1)S(1)}, u32[]{:S(2)}, u32[]{:S(2)}) collective-permute-start(bf16[1024,416]{0,1:T(8,128)(2,1)} %param.16), channel_id=1, source_target_pairs={{0,96},{32,0},{64,32},{96,64},{1,97},{33,1},{65,33},{97,65},{2,98}... | collective-permute-start | bytes 2555912 | tf_op jit(solution)/shard_map/ppermute | solution.py:44
  33.9 11.4 %collective-permute-start.2 = (bf16[512,416]{0,1:T(8,128)(2,1)S(1)}, bf16[512,416]{0,1:T(8,128)(2,1)S(1)}, u32[]{:S(2)}, u32[]{:S(2)}) collective-permute-start(bf16[512,416]{0,1:T(8,128)(2,1)S(1)} %slice.103), channel_id=1, source_target_pairs={{0,32},{32,64},{64,96},{96,0},{1,33},{33,65},{65,97},{97,1},{2,34}... | collective-permute-start | bytes 1277960 | tf_op jit(solution)/shard_map/ppermute | solution.py:45
  34.1 11.3 %collective-permute-start.3 = (bf16[512,416]{0,1:T(8,128)(2,1)S(1)}, bf16[512,416]{0,1:T(8,128)(2,1)S(1)}, u32[]{:S(2)}, u32[]{:S(2)}) collective-permute-start(bf16[512,416]{0,1:T(8,128)(2,1)S(1)} %slice.104), channel_id=1, source_target_pairs={{0,96},{32,0},{64,32},{96,64},{1,97},{33,1},{65,33},{97,65},{2,98}... | collective-permute-start | bytes 1277960 | tf_op jit(solution)/shard_map/ppermute | solution.py:46
  47.0 1.1 copy-start.1
  47.0 2.2 copy-start.2
  47.0 60.6 %copy-start.14 = (f32[1664]{0:T(1024)S(1)}, f32[1664]{0:T(1024)}, u32[]{:S(2)}) copy-start(f32[1664]{0:T(1024)} %param.19) | copy-start | bytes 19972
  47.0 60.6 %copy-start.15 = (f32[1664]{0:T(1024)S(1)}, f32[1664]{0:T(1024)}, u32[]{:S(2)}) copy-start(f32[1664]{0:T(1024)} %param.18) | copy-start | bytes 19972
  58.9 59.4 %copy-start.12 = (s32[1024]{0:T(1024)S(1)}, s32[1024]{0:T(1024)}, u32[]{:S(2)}) copy-start(s32[1024]{0:T(1024)} %param.17) | copy-start | bytes 12292
  150.4 12.5 %collective-permute-start.4 = (bf16[512,416]{0,1:T(8,128)(2,1)S(1)}, bf16[512,416]{0,1:T(8,128)(2,1)S(1)}, u32[]{:S(2)}, u32[]{:S(2)}) collective-permute-start(bf16[512,416]{0,1:T(8,128)(2,1)S(1)} %convolution_convert_fusion.2), channel_id=1, source_target_pairs={{0,32},{32,64},{64,96},{96,0},{1,33},{33,65},{65,97},{97,1},{2,34}... | collective-permute-start | bytes 1277960 | tf_op jit(solution)/shard_map/ppermute | solution.py:71
  152.2 11.3 %collective-permute-start.7 = (bf16[512,416]{0,1:T(8,128)(2,1)S(1)}, bf16[512,416]{0,1:T(8,128)(2,1)S(1)}, u32[]{:S(2)}, u32[]{:S(2)}) collective-permute-start(bf16[512,416]{0,1:T(8,128)(2,1)S(1)} %convolution_convert_fusion.1), channel_id=1, source_target_pairs={{0,96},{32,0},{64,32},{96,64},{1,97},{33,1},{65,33},{97,65},{2,98}... | collective-permute-start | bytes 1277960 | tf_op jit(solution)/shard_map/ppermute | solution.py:72
  163.3 22.8 %copy-start.3 = (bf16[1024,416]{0,1:T(8,128)(2,1)S(1)}, bf16[1024,416]{0,1:T(8,128)(2,1)}, u32[]{:S(2)}) copy-start(bf16[1024,416]{0,1:T(8,128)(2,1)} %param.16) | copy-start | bytes 2555908
  163.3 11.6 %collective-permute-start.5 = (bf16[512,416]{0,1:T(8,128)(2,1)S(1)}, bf16[512,416]{0,1:T(8,128)(2,1)S(1)}, u32[]{:S(2)}, u32[]{:S(2)}) collective-permute-start(bf16[512,416]{0,1:T(8,128)(2,1)S(1)} %add_convert_fusion.7), channel_id=1, source_target_pairs={{0,32},{32,64},{64,96},{96,0},{1,33},{33,65},{65,97},{97,1},{2,34}... | collective-permute-start | bytes 1277960 | tf_op jit(solution)/shard_map/ppermute | solution.py:71
  163.8 11.3 %collective-permute-start.8 = (bf16[512,416]{0,1:T(8,128)(2,1)S(1)}, bf16[512,416]{0,1:T(8,128)(2,1)S(1)}, u32[]{:S(2)}, u32[]{:S(2)}) collective-permute-start(bf16[512,416]{0,1:T(8,128)(2,1)S(1)} %add_convert_fusion.5), channel_id=1, source_target_pairs={{0,96},{32,0},{64,32},{96,64},{1,97},{33,1},{65,33},{97,65},{2,98}... | collective-permute-start | bytes 1277960 | tf_op jit(solution)/shard_map/ppermute | solution.py:72
  166.9 23.8 %copy-start.13 = (s32[256,1]{0,1:T(1,128)S(1)}, s32[256,1]{0,1:T(1,128)}, u32[]{:S(2)}) copy-start(s32[256,1]{0,1:T(1,128)} %param.29) | copy-start | bytes 3076
  175.1 10.8 %collective-permute-start.6 = (bf16[512,416]{0,1:T(8,128)(2,1)S(1)}, bf16[512,416]{0,1:T(8,128)(2,1)S(1)}, u32[]{:S(2)}, u32[]{:S(2)}) collective-permute-start(bf16[512,416]{0,1:T(8,128)(2,1)S(1)} %add_convert_fusion.6), channel_id=1, source_target_pairs={{0,32},{32,64},{64,96},{96,0},{1,33},{33,65},{65,97},{97,1},{2,34}... | collective-permute-start | bytes 1277960 | tf_op jit(solution)/shard_map/ppermute | solution.py:71
  175.3 10.7 %collective-permute-start.9 = (bf16[512,416]{0,1:T(8,128)(2,1)S(1)}, bf16[512,416]{0,1:T(8,128)(2,1)S(1)}, u32[]{:S(2)}, u32[]{:S(2)}) collective-permute-start(bf16[512,416]{0,1:T(8,128)(2,1)S(1)} %add_convert_fusion.4), channel_id=1, source_target_pairs={{0,96},{32,0},{64,32},{96,64},{1,97},{33,1},{65,33},{97,65},{2,98}... | collective-permute-start | bytes 1277960 | tf_op jit(solution)/shard_map/ppermute | solution.py:72
  186.4 19.1 %collective-permute-start.11 = (bf16[1024,416]{0,1:T(8,128)(2,1)S(1)}, bf16[1024,416]{0,1:T(8,128)(2,1)S(1)}, u32[]{:S(2)}, u32[]{:S(2)}) collective-permute-start(bf16[1024,416]{0,1:T(8,128)(2,1)S(1)} %fusion.71), channel_id=1, source_target_pairs={{0,32},{32,64},{64,96},{96,0},{1,33},{33,65},{65,97},{97,1},{2,34}... | collective-permute-start | bytes 2555912 | tf_op jit(solution)/shard_map/ppermute | solution.py:43
  186.5 19.4 %collective-permute-start.10 = (bf16[1024,416]{0,1:T(8,128)(2,1)S(1)}, bf16[1024,416]{0,1:T(8,128)(2,1)S(1)}, u32[]{:S(2)}, u32[]{:S(2)}) collective-permute-start(bf16[1024,416]{0,1:T(8,128)(2,1)S(1)} %fusion.71), channel_id=1, source_target_pairs={{0,96},{32,0},{64,32},{96,64},{1,97},{33,1},{65,33},{97,65},{2,98}... | collective-permute-start | bytes 2555912 | tf_op jit(solution)/shard_map/ppermute | solution.py:44
  205.5 9.2 %copy-start.4 = (bf16[1024,416]{0,1:T(8,128)(2,1)}, bf16[1024,416]{0,1:T(8,128)(2,1)S(1)}, u32[]{:S(2)}) copy-start(bf16[1024,416]{0,1:T(8,128)(2,1)S(1)} %collective-permute-done.11) | copy-start | bytes 2555908
  205.6 9.2 %collective-permute-start.12 = (bf16[512,416]{0,1:T(8,128)(2,1)S(1)}, bf16[512,416]{0,1:T(8,128)(2,1)S(1)}, u32[]{:S(2)}, u32[]{:S(2)}) collective-permute-start(bf16[512,416]{0,1:T(8,128)(2,1)S(1)} %slice.108), channel_id=1, source_target_pairs={{0,32},{32,64},{64,96},{96,0},{1,33},{33,65},{65,97},{97,1},{2,34}... | collective-permute-start | bytes 1277960 | tf_op jit(solution)/shard_map/ppermute | solution.py:45
  205.9 8.9 %copy-start.5 = (bf16[1024,416]{0,1:T(8,128)(2,1)}, bf16[1024,416]{0,1:T(8,128)(2,1)S(1)}, u32[]{:S(2)}) copy-start(bf16[1024,416]{0,1:T(8,128)(2,1)S(1)} %collective-permute-done.10) | copy-start | bytes 2555908
  205.9 8.8 %collective-permute-start.13 = (bf16[512,416]{0,1:T(8,128)(2,1)S(1)}, bf16[512,416]{0,1:T(8,128)(2,1)S(1)}, u32[]{:S(2)}, u32[]{:S(2)}) collective-permute-start(bf16[512,416]{0,1:T(8,128)(2,1)S(1)} %slice.109), channel_id=1, source_target_pairs={{0,96},{32,0},{64,32},{96,64},{1,97},{33,1},{65,33},{97,65},{2,98}... | collective-permute-start | bytes 1277960 | tf_op jit(solution)/shard_map/ppermute | solution.py:46
  216.7 0.9 copy-start
  230.6 8.8 %copy-start.16 = (f32[1664]{0:T(1024)S(1)}, f32[1664]{0:T(1024)}, u32[]{:S(2)}) copy-start(f32[1664]{0:T(1024)} %param.23) | copy-start | bytes 19972
  230.6 8.8 %copy-start.17 = (f32[1664]{0:T(1024)S(1)}, f32[1664]{0:T(1024)}, u32[]{:S(2)}) copy-start(f32[1664]{0:T(1024)} %param.22) | copy-start | bytes 19972
  280.2 7.4 %slice-start = ((s8[6815744]{0:T(1024)(128)(4,1)}), s8[4194304]{0:T(1024)(128)(4,1)S(1)}, s32[]{:S(2)}) async-start(s8[6815744]{0:T(1024)(128)(4,1)} %bitcast.246), calls=%async_computation.6 | async-start | bytes 8388608
  280.2 7.4 %copy-start.18 = (bf16[1024,2048]{1,0:T(8,128)(2,1)S(1)}, bf16[1024,2048]{1,0:T(8,128)(2,1)}, u32[]{:S(2)}) copy-start(bf16[1024,2048]{1,0:T(8,128)(2,1)} %fusion.26) | copy-start | bytes 12582916
  280.2 7.4 %slice-start.1 = ((s8[6815744]{0:T(1024)(128)(4,1)}), s8[2621440]{0:T(1024)(128)(4,1)S(1)}, s32[]{:S(2)}) async-start(s8[6815744]{0:T(1024)(128)(4,1)} %bitcast.246), calls=%async_computation.7 | async-start | bytes 5242880
  287.4 8.8 %collective-permute-start.14 = (bf16[512,416]{0,1:T(8,128)(2,1)S(1)}, bf16[512,416]{0,1:T(8,128)(2,1)S(1)}, u32[]{:S(2)}, u32[]{:S(2)}) collective-permute-start(bf16[512,416]{0,1:T(8,128)(2,1)S(1)} %fusion.113), channel_id=1, source_target_pairs={{0,32},{32,64},{64,96},{96,0},{1,33},{33,65},{65,97},{97,1},{2,34}... | collective-permute-start | bytes 1277960 | tf_op jit(solution)/shard_map/ppermute | solution.py:71
  288.7 8.7 %collective-permute-start.17 = (bf16[512,416]{0,1:T(8,128)(2,1)S(1)}, bf16[512,416]{0,1:T(8,128)(2,1)S(1)}, u32[]{:S(2)}, u32[]{:S(2)}) collective-permute-start(bf16[512,416]{0,1:T(8,128)(2,1)S(1)} %fusion.118), channel_id=1, source_target_pairs={{0,96},{32,0},{64,32},{96,64},{1,97},{33,1},{65,33},{97,65},{2,98}... | collective-permute-start | bytes 1277960 | tf_op jit(solution)/shard_map/ppermute | solution.py:72
  297.3 8.3 %collective-permute-start.15 = (bf16[512,416]{0,1:T(8,128)(2,1)S(1)}, bf16[512,416]{0,1:T(8,128)(2,1)S(1)}, u32[]{:S(2)}, u32[]{:S(2)}) collective-permute-start(bf16[512,416]{0,1:T(8,128)(2,1)S(1)} %add_convert_fusion.3), channel_id=1, source_target_pairs={{0,32},{32,64},{64,96},{96,0},{1,33},{33,65},{65,97},{97,1},{2,34}... | collective-permute-start | bytes 1277960 | tf_op jit(solution)/shard_map/ppermute | solution.py:71
  298.5 7.8 %collective-permute-start.18 = (bf16[512,416]{0,1:T(8,128)(2,1)S(1)}, bf16[512,416]{0,1:T(8,128)(2,1)S(1)}, u32[]{:S(2)}, u32[]{:S(2)}) collective-permute-start(bf16[512,416]{0,1:T(8,128)(2,1)S(1)} %add_convert_fusion.1), channel_id=1, source_target_pairs={{0,96},{32,0},{64,32},{96,64},{1,97},{33,1},{65,33},{97,65},{2,98}... | collective-permute-start | bytes 1277960 | tf_op jit(solution)/shard_map/ppermute | solution.py:72
  305.7 9.6 %collective-permute-start.16 = (bf16[512,416]{0,1:T(8,128)(2,1)S(1)}, bf16[512,416]{0,1:T(8,128)(2,1)S(1)}, u32[]{:S(2)}, u32[]{:S(2)}) collective-permute-start(bf16[512,416]{0,1:T(8,128)(2,1)S(1)} %add_convert_fusion.2), channel_id=1, source_target_pairs={{0,32},{32,64},{64,96},{96,0},{1,33},{33,65},{65,97},{97,1},{2,34}... | collective-permute-start | bytes 1277960 | tf_op jit(solution)/shard_map/ppermute | solution.py:71
  306.4 9.9 %collective-permute-start.19 = (bf16[512,416]{0,1:T(8,128)(2,1)S(1)}, bf16[512,416]{0,1:T(8,128)(2,1)S(1)}, u32[]{:S(2)}, u32[]{:S(2)}) collective-permute-start(bf16[512,416]{0,1:T(8,128)(2,1)S(1)} %add_convert_fusion), channel_id=1, source_target_pairs={{0,96},{32,0},{64,32},{96,64},{1,97},{33,1},{65,33},{97,65},{2,98}... | collective-permute-start | bytes 1277960 | tf_op jit(solution)/shard_map/ppermute | solution.py:72
  316.9 4.6 %collective-permute-start.20 = (f32[2,1024]{1,0:T(2,128)S(1)}, f32[2,1024]{1,0:T(2,128)S(1)}, u32[]{:S(2)}, u32[]{:S(2)}) collective-permute-start(f32[2,1024]{1,0:T(2,128)S(1)} %pad_maximum_fusion.2), channel_id=1, source_target_pairs={{0,96},{32,0},{64,32},{96,64},{1,97},{33,1},{65,33},{97,65},{2,98}... | collective-permute-start | bytes 24584 | tf_op jit(solution)/shard_map/ppermute | solution.py:88
  320.1 4.1 %collective-permute-start.21 = (f32[2,1024]{1,0:T(2,128)S(1)}, f32[2,1024]{1,0:T(2,128)S(1)}, u32[]{:S(2)}, u32[]{:S(2)}) collective-permute-start(f32[2,1024]{1,0:T(2,128)S(1)} %pad_maximum_fusion.2), channel_id=1, source_target_pairs={{0,64},{32,96},{64,0},{96,32},{1,65},{33,97},{65,1},{97,33},{2,66}... | collective-permute-start | bytes 24584 | tf_op jit(solution)/shard_map/ppermute | solution.py:88
  320.7 3.7 collective-permute-start.22
  325.9 5.6 %copy-start.11 = (bf16[4,416,1,416]{1,0,3,2:T(4,128)(2,1)S(1)}, bf16[4,416,1,416]{1,0,3,2:T(4,128)(2,1)}, u32[]{:S(2)}) copy-start(bf16[4,416,1,416]{1,0,3,2:T(4,128)(2,1)} %get-tuple-element.66) | copy-start | bytes 4153348
  325.9 6.3 %copy-start.10 = (bf16[4,416,1,416]{1,0,3,2:T(4,128)(2,1)S(1)}, bf16[4,416,1,416]{1,0,3,2:T(4,128)(2,1)}, u32[]{:S(2)}) copy-start(bf16[4,416,1,416]{1,0,3,2:T(4,128)(2,1)} %get-tuple-element.65) | copy-start | bytes 4153348
  326.8 8.7 %copy-start.9 = (bf16[4,416,1,416]{1,0,3,2:T(4,128)(2,1)S(1)}, bf16[4,416,1,416]{1,0,3,2:T(4,128)(2,1)}, u32[]{:S(2)}) copy-start(bf16[4,416,1,416]{1,0,3,2:T(4,128)(2,1)} %get-tuple-element.63) | copy-start | bytes 4153348
  326.9 9.2 %copy-start.8 = (bf16[4,416,1,416]{1,0,3,2:T(4,128)(2,1)S(1)}, bf16[4,416,1,416]{1,0,3,2:T(4,128)(2,1)}, u32[]{:S(2)}) copy-start(bf16[4,416,1,416]{1,0,3,2:T(4,128)(2,1)} %get-tuple-element.69) | copy-start | bytes 4153348
  329.1 7.6 %collective-permute-start.23 = (bf16[128,416]{0,1:T(8,128)(2,1)S(1)}, bf16[128,416]{0,1:T(8,128)(2,1)S(1)}, u32[]{:S(2)}, u32[]{:S(2)}) collective-permute-start(bf16[128,416]{0,1:T(8,128)(2,1)S(1)} %fusion.132), channel_id=1, source_target_pairs={{0,32},{32,64},{64,96},{96,0},{1,33},{33,65},{65,97},{97,1},{2,34}... | collective-permute-start | bytes 319496 | tf_op jit(solution)/shard_map/ppermute | solution.py:71
  329.2 7.6 %copy-start.7 = (bf16[4,416,1,416]{1,0,3,2:T(4,128)(2,1)S(1)}, bf16[4,416,1,416]{1,0,3,2:T(4,128)(2,1)}, u32[]{:S(2)}) copy-start(bf16[4,416,1,416]{1,0,3,2:T(4,128)(2,1)} %get-tuple-element.68) | copy-start | bytes 4153348
  331.4 6.2 %copy-start.6 = (bf16[4,416,1,416]{1,0,3,2:T(4,128)(2,1)S(1)}, bf16[4,416,1,416]{1,0,3,2:T(4,128)(2,1)}, u32[]{:S(2)}) copy-start(bf16[4,416,1,416]{1,0,3,2:T(4,128)(2,1)} %get-tuple-element.64) | copy-start | bytes 4153348
  332.8 4.8 %collective-permute-start.26 = (bf16[128,416]{0,1:T(8,128)(2,1)S(1)}, bf16[128,416]{0,1:T(8,128)(2,1)S(1)}, u32[]{:S(2)}, u32[]{:S(2)}) collective-permute-start(bf16[128,416]{0,1:T(8,128)(2,1)S(1)} %fusion.131), channel_id=1, source_target_pairs={{0,96},{32,0},{64,32},{96,64},{1,97},{33,1},{65,33},{97,65},{2,98}... | collective-permute-start | bytes 319496 | tf_op jit(solution)/shard_map/ppermute | solution.py:72
  337.5 5.3 %collective-permute-start.24 = (bf16[128,416]{0,1:T(8,128)(2,1)S(1)}, bf16[128,416]{0,1:T(8,128)(2,1)S(1)}, u32[]{:S(2)}, u32[]{:S(2)}) collective-permute-start(bf16[128,416]{0,1:T(8,128)(2,1)S(1)} %add_convert_fusion.13), channel_id=1, source_target_pairs={{0,32},{32,64},{64,96},{96,0},{1,33},{33,65},{65,97},{97,1},{2,34}... | collective-permute-start | bytes 319496 | tf_op jit(solution)/shard_map/ppermute | solution.py:71
  338.3 4.6 %collective-permute-start.27 = (bf16[128,416]{0,1:T(8,128)(2,1)S(1)}, bf16[128,416]{0,1:T(8,128)(2,1)S(1)}, u32[]{:S(2)}, u32[]{:S(2)}) collective-permute-start(bf16[128,416]{0,1:T(8,128)(2,1)S(1)} %add_convert_fusion.10), channel_id=1, source_target_pairs={{0,96},{32,0},{64,32},{96,64},{1,97},{33,1},{65,33},{97,65},{2,98}... | collective-permute-start | bytes 319496 | tf_op jit(solution)/shard_map/ppermute | solution.py:72
  342.8 4.8 %collective-permute-start.25 = (bf16[128,416]{0,1:T(8,128)(2,1)S(1)}, bf16[128,416]{0,1:T(8,128)(2,1)S(1)}, u32[]{:S(2)}, u32[]{:S(2)}) collective-permute-start(bf16[128,416]{0,1:T(8,128)(2,1)S(1)} %add_convert_fusion.12), channel_id=1, source_target_pairs={{0,32},{32,64},{64,96},{96,0},{1,33},{33,65},{65,97},{97,1},{2,34}... | collective-permute-start | bytes 319496 | tf_op jit(solution)/shard_map/ppermute | solution.py:71
  342.9 5.0 %collective-permute-start.28 = (bf16[128,416]{0,1:T(8,128)(2,1)S(1)}, bf16[128,416]{0,1:T(8,128)(2,1)S(1)}, u32[]{:S(2)}, u32[]{:S(2)}) collective-permute-start(bf16[128,416]{0,1:T(8,128)(2,1)S(1)} %add_convert_fusion.9), channel_id=1, source_target_pairs={{0,96},{32,0},{64,32},{96,64},{1,97},{33,1},{65,33},{97,65},{2,98}... | collective-permute-start | bytes 319496 | tf_op jit(solution)/shard_map/ppermute | solution.py:72
Sparse Core Ops, SparseCore 0:
  9.6 46.5 all-gather.12
  58.5 49.1 all-gather.8
  109.9 48.5 all-gather.10
  160.6 49.5 all-gather.14
  212.3 49.7 all-gather.16

commit v2 on v1

--- a/solution.py
+++ b/solution.py
@@ -56,6 +56,28 @@
     return jnp.concatenate(columns, axis=1)
 
 
+def gx_reduce_scatter(y, n):
+    me = lax.axis_index("gx")
+    rows = y.shape[0]
+    width = y.shape[1] // n
+    half = rows // 2
+    blocks = y.reshape(rows, n, width)
+
+    def own(part, index):
+        return lax.dynamic_slice_in_dim(part, index % n, 1, axis=1)[:, 0]
+
+    top = blocks[:half]
+    bottom = blocks[half:]
+    acc_top = own(top, me - 1)
+    acc_bottom = own(bottom, me + 1)
+    for step in range(1, n):
+        got_top = lax.ppermute(acc_top.astype(jnp.bfloat16), "gx", ring_perm(n, 1))
+        got_bottom = lax.ppermute(acc_bottom.astype(jnp.bfloat16), "gx", ring_perm(n, -1))
+        acc_top = got_top.astype(jnp.float32) + own(top, me - step - 1)
+        acc_bottom = got_bottom.astype(jnp.float32) + own(bottom, me + step + 1)
+    return jnp.concatenate([acc_top, acc_bottom], axis=0)
+
+
 def gx_matmul_reduce_scatter(lhs, w_blocks, contract, n):
     me = lax.axis_index("gx")
     half = lhs.shape[0] // 2
@@ -100,7 +122,7 @@
     queries = qkv[0].reshape(tok_rows, head_count, HEAD)
     key_rows = qkv[1].reshape(tok_rows, head_count, HEAD)
     value_rows = qkv[2].reshape(tok_rows, head_count, HEAD)
-    query_block = min(512, tok_rows)
+    query_block = tok_rows
 
     def one_block(index):
         first_query = index * query_block
@@ -150,9 +172,6 @@
     width = feature_cols
     proj_blocks = proj_all.reshape(proj_all.shape[0], n_gx, width).transpose(1, 0, 2)
     down_blocks = down_all.reshape(down_all.shape[0], n_gx, width).transpose(1, 0, 2)
-    merge_blocks = merge_all.reshape(
-        merge_all.shape[0], merge_all.shape[1], n_gx, width
-    ).transpose(2, 0, 1, 3)
     full_rows = gx_all_gather(tokens, n_gx)
     normed = normalize_rows(full_rows, first_gain, first_bias).astype(jnp.bfloat16)
     columns = normed
@@ -190,9 +209,8 @@
         .transpose(0, 2, 1, 3, 4)
         .reshape(merged_rows, 4, feature_cols)
     )
-    projected = gx_matmul_reduce_scatter(grouped, merge_blocks, merge_dot, n_gx).astype(
-        jnp.bfloat16
-    )
+    merge_terms = merge_dot(grouped, merge_all)
+    projected = gx_reduce_scatter(merge_terms, n_gx).astype(jnp.bfloat16)
     owner_count = lax.axis_size("gy")
     capacity = max(2, 2 * merged_rows // owner_count)
     owner_col = owners[:, 0]

time: 390 us -> 356 us (0.913)
  matrix products: 93.7 us -> 74.7 us
  local copies, waits for them, and re-layouts: 43.2 us -> 28.8 us
    another operation x2 -> x1, local copies, waits for them, and re-layouts: 12 us -> 0.01 us
    ppermute x0 -> x6, starting transfers between devices: none -> 8.97 us  [the longest x3 8.74 us: gx_reduce_scatter(): lax.ppermute(acc_bottom.astype(jnp.bfloat16), 'gx', ring_perm(n, -1))]
    ppermute x9 -> x6, starting transfers between devices: 24.2 us -> 16.2 us  [gx_matmul_reduce_scatter(): lax.ppermute(acc_bottom.astype(jnp.bfloat16), 'gx', ring_perm(n, -1))]
    ppermute x9 -> x6, waiting for transfers between devices: 38.8 us -> 32.4 us  [gx_matmul_reduce_scatter(): got_top = lax.ppermute(acc_top.astype(jnp.bfloat16), 'gx', ring_perm(n, 1))]
    ppermute x0 -> x6, waiting for transfers between devices: none -> 6.23 us  [the longest x3 6.23 us: gx_reduce_scatter(): got_top = lax.ppermute(acc_top.astype(jnp.bfloat16), 'gx', ring_perm(n, 1))]
    dot_general x16, matrix products: 16.7 us -> 11.6 us  [plain_dot(): return jnp.dot(lhs, rhs, preferred_element_type=jnp.float32)]
    dot_general x2 -> x1, matrix products: 11.7 us -> 7.17 us  [one_block(): jnp.einsum('hqk,khe->qhe', shares, value_rows, preferred_element_type=jnp...]
    sub x2 -> x1, matrix products: 15.3 us -> 11.4 us  [one_block(): raised = jnp.exp(scores - highest)]
  transfers between devices with their start and end apart: 34 -> 34, of which waited for: 19 -> 20; matrix products, arithmetic and copies ran while one was open for 32% -> 31% of each run, Pallas kernels for 0% -> 0%
where the time goes in v2:
time: 356 us; the launch traced here: 352 us
  waiting for transfers between devices  149 us (42%)
  matrix products  74.7 us (21%)
  starting transfers between devices  45 us (13%)
  local copies, waits for them, and re-layouts  28.8 us (8%)
  blocking collectives  28.2 us (8%)
  between operations  14.4 us (4%)
  other arithmetic  12.4 us (3%)
    all_gather x1, waiting for transfers between devices, body(): qkv_all = lax.all_gather(query_key_value, 'gy', axis=1, tiled=True)  48.7 us
    ppermute x2, waiting for transfers between devices, gx_all_gather(): from_left = lax.ppermute(x, 'gx', ring_perm(n, 1))  32.9 us
    ppermute x6, waiting for transfers between devices, gx_matmul_reduce_scatter(): got_top = lax.ppermute(acc_top.astype(jnp.bfloat16), 'gx', ring_perm(n, 1))  32.4 us
    dot_general x1, matrix products, body(): upper = jnp.dot(columns, up_all, preferred_element_type=jnp.float32)  29.5 us
    all_to_all x1, blocking collectives, body(): lax.all_to_all(outgoing, 'gy', split_axis=0, concat_axis=0, tiled=True)  28.2 us
    unnamed x36, local copies, waits for them, and re-layouts  23.4 us
    ppermute x6, starting transfers between devices, gx_matmul_reduce_scatter(): lax.ppermute(acc_bottom.astype(jnp.bfloat16), 'gx', ring_perm(n, -1))  16.2 us
    ppermute x2, waiting for transfers between devices, gx_all_gather(): far_top = lax.ppermute(from_left[:half], 'gx', ring_perm(n, 1))  12.1 us
  transfers between devices with their start and end apart: 34, of which 20 were waited for; matrix products, arithmetic and copies ran while one was open for 31% of the time, Pallas kernels for 0%

profile of v2, /device:TPU:1, one launch (start us, length us, event | category | flops | bytes accessed | tf_op | source)
XLA Modules:
  0.0 352.4 jit_solution(16357987010700719370)
XLA Ops:
  6.5 0.7 all-gather.13.cloned.1.call-update
  7.3 1.7 copy.32
  10.4 2.5 collective-permute-start.1
  12.9 2.2 collective-permute-start
  15.1 18.8 %collective-permute-done.1 = bf16[1024,416]{0,1:T(8,128)(2,1)S(1)} collective-permute-done((bf16[1024,416]{0,1:T(8,128)(2,1)}, bf16[1024,416]{0,1:T(8,128)(2,1)S(1)}, u32[]{:S(2)}, u32[]{:S(2)}) %collective-permute-start.1) | collective-permute-done | bytes 852000 | tf_op jit(solution)/shard_map/ppermute | solution.py:43
  34.1 2.7 collective-permute-start.3
  36.8 2.4 broadcast_compare_fusion
  39.2 6.1 %collective-permute-done.2 = bf16[512,416]{0,1:T(8,128)(2,1)S(1)} collective-permute-done((bf16[512,416]{0,1:T(8,128)(2,1)S(1)}, bf16[512,416]{0,1:T(8,128)(2,1)S(1)}, u32[]{:S(2)}, u32[]{:S(2)}) %collective-permute-start.2) | collective-permute-done | bytes 426016 | tf_op jit(solution)/shard_map/ppermute | solution.py:45
  45.4 1.6 select_select_fusion.7
  47.1 0.8 convert_reduce_fusion.1
  47.9 1.0 fusion.24
  49.0 7.2 %all-gather.13.cloned.1.call-done = bf16[32,52,416]{2,1,0:T(8,128)(2,1)} async-done(((bf16[1,52,416]{2,1,0:T(8,128)(2,1)}), bf16[32,52,416]{2,1,0:T(8,128)(2,1)}) %all-gather.13.cloned.1.call-update) | async-done | bytes 1384464 | tf_op jit(solution)/shard_map/all_gather | solution.py:168
  56.2 2.7 reshape.193
  58.9 48.7 %all-gather.9.cloned.1.call-done = bf16[3,1664,416]{2,0,1:T(4,128)(2,1)} async-done(((bf16[3,52,416]{2,0,1:T(4,128)(2,1)}), bf16[3,1664,416]{2,0,1:T(4,128)(2,1)}) %all-gather.9.cloned.1.call-update) | async-done | bytes 4153360 | tf_op jit(solution)/shard_map/all_gather | solution.py:167
  107.6 9.2 %convert_bitcast_fusion = bf16[3,1024,416]{1,2,0:T(8,128)(2,1)S(1)} fusion(bf16[3,1664,416]{2,0,1:T(4,128)(2,1)} %all-gather.9.cloned.1.call-done, f32[1664]{0:T(1024)S(1)} %copy-done.8, f32[1664]{0:T(1024)S(1)} %copy-done.9, f32[1024]{0:T(1024)S(1)} %add_rsqrt_fusion.2, f32[1024]{0:T(1024)S(1)} %broadcast_multiply_fusion.1, ...), kind=kOutput, calls=%fused_computation.64 | convolution fusion | flops 4276453376 | bytes 10138624 | tf_op jit(solution)/shard_map/td,kdc->ktc/dot_general | solution.py:178
  116.9 1.2 fusion.175
  118.0 11.4 %fusion.178 = (f32[4,1024]{1,0:T(4,128)S(1)}, f32[4,1024,1024]{1,2,0:T(8,128)}) fusion(pred[1024,1024]{0,1:T(8,128)(4,1)} %broadcast_compare_fusion, bf16[1024,4,104]{0,2,1:T(8,128)(2,1)} %bitcast.209, bf16[1024,4,104]{0,2,1:T(8,128)(2,1)S(1)} %bitcast.208), kind=kOutput, calls=%fused_computation.232 | convolution fusion | flops 889193472 | bytes 19546112 | tf_op jit(solution)/shard_map/while/body/eval_jaxpr/sub | solution.py:137
  129.4 7.2 %fusion.95 = bf16[1024,4,104]{0,2,1:T(8,128)(2,1)S(1)} fusion(bf16[1024,4,104]{0,2,1:T(8,128)(2,1)S(1)} %bitcast.207, f32[4,1024,1024]{1,2,0:T(8,128)} %get-tuple-element.44, f32[4,1024]{1,0:T(4,128)S(1)} %get-tuple-element.43), kind=kOutput, calls=%fused_computation.109 | convolution fusion | flops 881229824 | bytes 18497536 | tf_op jit(solution)/shard_map/while/body/eval_jaxpr/hqk,khe->qhe/dot_general | solution.py:139
  137.1 1.6 collective-permute-start.4
  139.0 1.5 collective-permute-start.7
  141.3 8.5 %collective-permute-done.4 = bf16[512,416]{0,1:T(8,128)(2,1)S(1)} collective-permute-done((bf16[512,416]{0,1:T(8,128)(2,1)S(1)}, bf16[512,416]{0,1:T(8,128)(2,1)S(1)}, u32[]{:S(2)}, u32[]{:S(2)}) %collective-permute-start.4) | collective-permute-done | bytes 426016 | tf_op jit(solution)/shard_map/ppermute | solution.py:93
  150.7 2.7 collective-permute-start.8
  153.8 8.0 %collective-permute-done.5 = bf16[512,416]{0,1:T(8,128)(2,1)S(1)} collective-permute-done((bf16[512,416]{0,1:T(8,128)(2,1)S(1)}, bf16[512,416]{0,1:T(8,128)(2,1)S(1)}, u32[]{:S(2)}, u32[]{:S(2)}) %collective-permute-start.5) | collective-permute-done | bytes 426016 | tf_op jit(solution)/shard_map/ppermute | solution.py:93
  162.2 2.7 collective-permute-start.9
  165.3 7.4 %collective-permute-done.6 = bf16[512,416]{0,1:T(8,128)(2,1)S(1)} collective-permute-done((bf16[512,416]{0,1:T(8,128)(2,1)S(1)}, bf16[512,416]{0,1:T(8,128)(2,1)S(1)}, u32[]{:S(2)}, u32[]{:S(2)}) %collective-permute-start.6) | collective-permute-done | bytes 426016 | tf_op jit(solution)/shard_map/ppermute | solution.py:93
  173.4 2.7 collective-permute-start.10
  176.1 0.8 dynamic_slice.59
  176.9 0.8 dynamic_slice.60
  178.2 14.1 %collective-permute-done.11 = bf16[1024,416]{0,1:T(8,128)(2,1)S(1)} collective-permute-done((bf16[1024,416]{0,1:T(8,128)(2,1)S(1)}, bf16[1024,416]{0,1:T(8,128)(2,1)S(1)}, u32[]{:S(2)}, u32[]{:S(2)}) %collective-permute-start.11) | collective-permute-done | bytes 852000 | tf_op jit(solution)/shard_map/ppermute | solution.py:43
  192.7 2.7 collective-permute-start.13
  195.6 6.0 %collective-permute-done.12 = bf16[512,416]{0,1:T(8,128)(2,1)S(1)} collective-permute-done((bf16[512,416]{0,1:T(8,128)(2,1)S(1)}, bf16[512,416]{0,1:T(8,128)(2,1)S(1)}, u32[]{:S(2)}, u32[]{:S(2)}) %collective-permute-start.12) | collective-permute-done | bytes 426016 | tf_op jit(solution)/shard_map/ppermute | solution.py:45
  201.7 1.9 select_select_fusion.3
  204.5 1.0 fusion.20
  205.5 8.7 %reshape.195 = bf16[1664,2048]{1,0:T(8,128)(2,1)} reshape(bf16[32,52,2048]{2,1,0:T(8,128)(2,1)} %all-gather.15.cloned.1.call-done) | data formatting | bytes 13631488
  214.2 9.0 %reshape.197 = bf16[1664,2048]{1,0:T(8,128)(2,1)} reshape(bf16[32,52,2048]{2,1,0:T(8,128)(2,1)} %all-gather.17.cloned.1.call-done) | data formatting | bytes 13631488
  223.3 29.5 %fusion.4 = bf16[1024,2048]{1,0:T(8,128)(2,1)S(1)} fusion(bf16[1664,2048]{1,0:T(8,128)(2,1)} %reshape.195, f32[1664]{0:T(1024)S(1)} %copy-done.10, f32[1664]{0:T(1024)S(1)} %copy-done.11, f32[1024]{0:T(1024)S(1)} %add_rsqrt_fusion.1, f32[1024]{0:T(1024)S(1)} %broadcast_multiply_fusion, bf16[1024,416]{0,1:T(8,128)(2,1)S(1)} %get-tuple-element.26, ...), kind=kOutput, calls=%fused_computation.12 | convolution fusion | flops 7137787904 | bytes 14439424 | tf_op jit(solution)/shard_map/dot_general | solution.py:190
  252.8 1.1 fusion.96
  254.0 1.1 fusion.101
  255.0 1.1 fusion.72
  256.1 2.7 collective-permute-start.17
  258.9 1.1 fusion.70
  259.9 2.2 collective-permute-done.14
  262.1 1.1 add_convert_fusion.3
  263.9 1.1 add_convert_fusion.1
  265.0 3.2 collective-permute-start.18
  268.2 1.1 fusion.64
  269.3 2.3 collective-permute-done.15
  271.8 1.8 collective-permute-done.18
  273.8 3.4 collective-permute-start.19
  277.2 1.1 fusion.62
  278.3 4.0 %collective-permute-done.16 = bf16[512,416]{0,1:T(8,128)(2,1)S(1)} collective-permute-done((bf16[512,416]{0,1:T(8,128)(2,1)S(1)}, bf16[512,416]{0,1:T(8,128)(2,1)S(1)}, u32[]{:S(2)}, u32[]{:S(2)}) %collective-permute-start.16) | collective-permute-done | bytes 426016 | tf_op jit(solution)/shard_map/ppermute | solution.py:93
  282.4 2.0 collective-permute-done.19
  285.0 3.2 collective-permute-start.20
  288.8 0.8 collective-permute-start.22
  289.6 2.7 collective-permute-done.21
  294.2 5.5 %fusion.46 = f32[256,1664]{1,0:T(8,128)S(1)} fusion(bf16[256,4,416]{2,0,1:T(8,128)(2,1)S(1)} %bitcast.206, bf16[4,416,1664]{1,0,2:T(4,128)(2,1)} %all-gather.11.cloned.1.call-done), kind=kOutput, calls=%fused_computation.60 | convolution fusion | flops 1417674752 | bytes 8093696 | tf_op jit(solution)/shard_map/pkf,kfc->pc/dot_general | solution.py:105
  300.5 2.7 collective-permute-start.26
  303.2 1.7 collective-permute-done.23
  305.1 3.0 collective-permute-start.27
  308.1 1.7 collective-permute-done.24
  310.0 3.0 collective-permute-start.28
  313.0 2.8 collective-permute-done.25
  316.4 28.2 %all_to_all.5 = bf16[32,16,416]{2,1,0:T(8,128)(2,1)S(1)} all-to-all(bf16[32,16,416]{2,1,0:T(8,128)(2,1)S(1)} %bitcast.204), channel_id=1, replica_groups=mesh['gx'=4,'gy'=32] {'gy'}, dimensions={0} | all-to-all | bytes 851968 | tf_op jit(solution)/shard_map/all_to_all | solution.py:228
  344.7 0.8 copy.67
  (129 shorter events, 13.8 us)
Async XLA Ops:
  6.5 49.7 %all-gather.13.cloned.1.call-start = ((), (), s32[]{:S(2)}) async-start(), calls=%async_computation.3 | async-start | bytes 1892352 | tf_op jit(solution)/shard_map/all_gather | solution.py:168
  7.3 100.4 %all-gather.9.cloned.1.call-start = ((), (), s32[]{:S(2)}) async-start(), calls=%async_computation.1 | async-start | bytes 7028736 | tf_op jit(solution)/shard_map/all_gather | solution.py:167
  9.0 196.5 %all-gather.15.cloned.1.call-start = ((), (), s32[]{:S(2)}) async-start(), calls=%async_computation.4 | async-start | bytes 7569408 | tf_op jit(solution)/shard_map/all_gather | solution.py:169
  9.8 204.4 %all-gather.17.cloned.1.call-start = ((), (), s32[]{:S(2)}) async-start(), calls=%async_computation.5 | async-start | bytes 7569408 | tf_op jit(solution)/shard_map/all_gather | solution.py:170
  10.4 283.8 %all-gather.11.cloned.1.call-start = ((), (), s32[]{:S(2)}) async-start(), calls=%async_computation.2 | async-start | bytes 7028736 | tf_op jit(solution)/shard_map/all_gather | solution.py:171
  10.4 23.5 %collective-permute-start.1 = (bf16[1024,416]{0,1:T(8,128)(2,1)}, bf16[1024,416]{0,1:T(8,128)(2,1)S(1)}, u32[]{:S(2)}, u32[]{:S(2)}) collective-permute-start(bf16[1024,416]{0,1:T(8,128)(2,1)} %param.14), channel_id=1, source_target_pairs={{0,32},{32,64},{64,96},{96,0},{1,33},{33,65},{65,97},{97,1},{2,34}... | collective-permute-start | bytes 2555912 | tf_op jit(solution)/shard_map/ppermute | solution.py:43
  12.9 21.1 %collective-permute-start = (bf16[1024,416]{0,1:T(8,128)(2,1)}, bf16[1024,416]{0,1:T(8,128)(2,1)S(1)}, u32[]{:S(2)}, u32[]{:S(2)}) collective-permute-start(bf16[1024,416]{0,1:T(8,128)(2,1)} %param.14), channel_id=1, source_target_pairs={{0,96},{32,0},{64,32},{96,64},{1,97},{33,1},{65,33},{97,65},{2,98}... | collective-permute-start | bytes 2555912 | tf_op jit(solution)/shard_map/ppermute | solution.py:44
  33.9 11.4 %collective-permute-start.2 = (bf16[512,416]{0,1:T(8,128)(2,1)S(1)}, bf16[512,416]{0,1:T(8,128)(2,1)S(1)}, u32[]{:S(2)}, u32[]{:S(2)}) collective-permute-start(bf16[512,416]{0,1:T(8,128)(2,1)S(1)} %slice.103), channel_id=1, source_target_pairs={{0,32},{32,64},{64,96},{96,0},{1,33},{33,65},{65,97},{97,1},{2,34}... | collective-permute-start | bytes 1277960 | tf_op jit(solution)/shard_map/ppermute | solution.py:45
  34.1 11.3 %collective-permute-start.3 = (bf16[512,416]{0,1:T(8,128)(2,1)S(1)}, bf16[512,416]{0,1:T(8,128)(2,1)S(1)}, u32[]{:S(2)}, u32[]{:S(2)}) collective-permute-start(bf16[512,416]{0,1:T(8,128)(2,1)S(1)} %slice.104), channel_id=1, source_target_pairs={{0,96},{32,0},{64,32},{96,64},{1,97},{33,1},{65,33},{97,65},{2,98}... | collective-permute-start | bytes 1277960 | tf_op jit(solution)/shard_map/ppermute | solution.py:46
  47.0 0.9 copy-start.1
  47.0 1.9 copy-start.2
  47.0 60.6 %copy-start.8 = (f32[1664]{0:T(1024)S(1)}, f32[1664]{0:T(1024)}, u32[]{:S(2)}) copy-start(f32[1664]{0:T(1024)} %param.17) | copy-start | bytes 19972
  47.0 60.6 %copy-start.9 = (f32[1664]{0:T(1024)S(1)}, f32[1664]{0:T(1024)}, u32[]{:S(2)}) copy-start(f32[1664]{0:T(1024)} %param.16) | copy-start | bytes 19972
  137.1 12.7 %collective-permute-start.4 = (bf16[512,416]{0,1:T(8,128)(2,1)S(1)}, bf16[512,416]{0,1:T(8,128)(2,1)S(1)}, u32[]{:S(2)}, u32[]{:S(2)}) collective-permute-start(bf16[512,416]{0,1:T(8,128)(2,1)S(1)} %convolution_convert_fusion.2), channel_id=1, source_target_pairs={{0,32},{32,64},{64,96},{96,0},{1,33},{33,65},{65,97},{97,1},{2,34}... | collective-permute-start | bytes 1277960 | tf_op jit(solution)/shard_map/ppermute | solution.py:93
  139.0 11.3 %collective-permute-start.7 = (bf16[512,416]{0,1:T(8,128)(2,1)S(1)}, bf16[512,416]{0,1:T(8,128)(2,1)S(1)}, u32[]{:S(2)}, u32[]{:S(2)}) collective-permute-start(bf16[512,416]{0,1:T(8,128)(2,1)S(1)} %convolution_convert_fusion.1), channel_id=1, source_target_pairs={{0,96},{32,0},{64,32},{96,64},{1,97},{33,1},{65,33},{97,65},{2,98}... | collective-permute-start | bytes 1277960 | tf_op jit(solution)/shard_map/ppermute | solution.py:94
  150.2 22.8 %copy-start.4 = (bf16[1024,416]{0,1:T(8,128)(2,1)S(1)}, bf16[1024,416]{0,1:T(8,128)(2,1)}, u32[]{:S(2)}) copy-start(bf16[1024,416]{0,1:T(8,128)(2,1)} %param.14) | copy-start | bytes 2555908
  150.2 11.6 %collective-permute-start.5 = (bf16[512,416]{0,1:T(8,128)(2,1)S(1)}, bf16[512,416]{0,1:T(8,128)(2,1)S(1)}, u32[]{:S(2)}, u32[]{:S(2)}) collective-permute-start(bf16[512,416]{0,1:T(8,128)(2,1)S(1)} %add_convert_fusion.7), channel_id=1, source_target_pairs={{0,32},{32,64},{64,96},{96,0},{1,33},{33,65},{65,97},{97,1},{2,34}... | collective-permute-start | bytes 1277960 | tf_op jit(solution)/shard_map/ppermute | solution.py:93
  150.7 11.3 %collective-permute-start.8 = (bf16[512,416]{0,1:T(8,128)(2,1)S(1)}, bf16[512,416]{0,1:T(8,128)(2,1)S(1)}, u32[]{:S(2)}, u32[]{:S(2)}) collective-permute-start(bf16[512,416]{0,1:T(8,128)(2,1)S(1)} %add_convert_fusion.5), channel_id=1, source_target_pairs={{0,96},{32,0},{64,32},{96,64},{1,97},{33,1},{65,33},{97,65},{2,98}... | collective-permute-start | bytes 1277960 | tf_op jit(solution)/shard_map/ppermute | solution.py:94
  153.8 23.8 %copy-start.7 = (s32[256,1]{0,1:T(1,128)S(1)}, s32[256,1]{0,1:T(1,128)}, u32[]{:S(2)}) copy-start(s32[256,1]{0,1:T(1,128)} %param.27) | copy-start | bytes 3076
  162.0 10.8 %collective-permute-start.6 = (bf16[512,416]{0,1:T(8,128)(2,1)S(1)}, bf16[512,416]{0,1:T(8,128)(2,1)S(1)}, u32[]{:S(2)}, u32[]{:S(2)}) collective-permute-start(bf16[512,416]{0,1:T(8,128)(2,1)S(1)} %add_convert_fusion.6), channel_id=1, source_target_pairs={{0,32},{32,64},{64,96},{96,0},{1,33},{33,65},{65,97},{97,1},{2,34}... | collective-permute-start | bytes 1277960 | tf_op jit(solution)/shard_map/ppermute | solution.py:93
  162.2 10.7 %collective-permute-start.9 = (bf16[512,416]{0,1:T(8,128)(2,1)S(1)}, bf16[512,416]{0,1:T(8,128)(2,1)S(1)}, u32[]{:S(2)}, u32[]{:S(2)}) collective-permute-start(bf16[512,416]{0,1:T(8,128)(2,1)S(1)} %add_convert_fusion.4), channel_id=1, source_target_pairs={{0,96},{32,0},{64,32},{96,64},{1,97},{33,1},{65,33},{97,65},{2,98}... | collective-permute-start | bytes 1277960 | tf_op jit(solution)/shard_map/ppermute | solution.py:94
  173.3 19.0 %collective-permute-start.11 = (bf16[1024,416]{0,1:T(8,128)(2,1)S(1)}, bf16[1024,416]{0,1:T(8,128)(2,1)S(1)}, u32[]{:S(2)}, u32[]{:S(2)}) collective-permute-start(bf16[1024,416]{0,1:T(8,128)(2,1)S(1)} %fusion.60), channel_id=1, source_target_pairs={{0,32},{32,64},{64,96},{96,0},{1,33},{33,65},{65,97},{97,1},{2,34}... | collective-permute-start | bytes 2555912 | tf_op jit(solution)/shard_map/ppermute | solution.py:43
  173.4 19.3 %collective-permute-start.10 = (bf16[1024,416]{0,1:T(8,128)(2,1)S(1)}, bf16[1024,416]{0,1:T(8,128)(2,1)S(1)}, u32[]{:S(2)}, u32[]{:S(2)}) collective-permute-start(bf16[1024,416]{0,1:T(8,128)(2,1)S(1)} %fusion.60), channel_id=1, source_target_pairs={{0,96},{32,0},{64,32},{96,64},{1,97},{33,1},{65,33},{97,65},{2,98}... | collective-permute-start | bytes 2555912 | tf_op jit(solution)/shard_map/ppermute | solution.py:44
  192.3 9.3 %copy-start.5 = (bf16[1024,416]{0,1:T(8,128)(2,1)}, bf16[1024,416]{0,1:T(8,128)(2,1)S(1)}, u32[]{:S(2)}) copy-start(bf16[1024,416]{0,1:T(8,128)(2,1)S(1)} %collective-permute-done.11) | copy-start | bytes 2555908
  192.4 9.2 %collective-permute-start.12 = (bf16[512,416]{0,1:T(8,128)(2,1)S(1)}, bf16[512,416]{0,1:T(8,128)(2,1)S(1)}, u32[]{:S(2)}, u32[]{:S(2)}) collective-permute-start(bf16[512,416]{0,1:T(8,128)(2,1)S(1)} %slice.110), channel_id=1, source_target_pairs={{0,32},{32,64},{64,96},{96,0},{1,33},{33,65},{65,97},{97,1},{2,34}... | collective-permute-start | bytes 1277960 | tf_op jit(solution)/shard_map/ppermute | solution.py:45
  192.7 8.9 %copy-start.6 = (bf16[1024,416]{0,1:T(8,128)(2,1)}, bf16[1024,416]{0,1:T(8,128)(2,1)S(1)}, u32[]{:S(2)}) copy-start(bf16[1024,416]{0,1:T(8,128)(2,1)S(1)} %collective-permute-done.10) | copy-start | bytes 2555908
  192.7 8.9 %collective-permute-start.13 = (bf16[512,416]{0,1:T(8,128)(2,1)S(1)}, bf16[512,416]{0,1:T(8,128)(2,1)S(1)}, u32[]{:S(2)}, u32[]{:S(2)}) collective-permute-start(bf16[512,416]{0,1:T(8,128)(2,1)S(1)} %slice.111), channel_id=1, source_target_pairs={{0,96},{32,0},{64,32},{96,64},{1,97},{33,1},{65,33},{97,65},{2,98}... | collective-permute-start | bytes 1277960 | tf_op jit(solution)/shard_map/ppermute | solution.py:46
  203.6 0.9 copy-start
  214.2 9.0 %copy-start.10 = (f32[1664]{0:T(1024)S(1)}, f32[1664]{0:T(1024)}, u32[]{:S(2)}) copy-start(f32[1664]{0:T(1024)} %param.21) | copy-start | bytes 19972
  214.2 9.1 %copy-start.11 = (f32[1664]{0:T(1024)S(1)}, f32[1664]{0:T(1024)}, u32[]{:S(2)}) copy-start(f32[1664]{0:T(1024)} %param.20) | copy-start | bytes 19972
  223.3 29.5 %copy-start.3 = (bf16[1664,2048]{1,0:T(8,128)(2,1)S(1)}, bf16[1664,2048]{1,0:T(8,128)(2,1)}, u32[]{:S(2)}) copy-start(bf16[1664,2048]{1,0:T(8,128)(2,1)} %reshape.197) | copy-start | bytes 20447236
  253.9 8.3 %collective-permute-start.14 = (bf16[512,416]{0,1:T(8,128)(2,1)S(1)}, bf16[512,416]{0,1:T(8,128)(2,1)S(1)}, u32[]{:S(2)}, u32[]{:S(2)}) collective-permute-start(bf16[512,416]{0,1:T(8,128)(2,1)S(1)} %fusion.96), channel_id=1, source_target_pairs={{0,32},{32,64},{64,96},{96,0},{1,33},{33,65},{65,97},{97,1},{2,34}... | collective-permute-start | bytes 1277960 | tf_op jit(solution)/shard_map/ppermute | solution.py:93
  256.1 7.8 %collective-permute-start.17 = (bf16[512,416]{0,1:T(8,128)(2,1)S(1)}, bf16[512,416]{0,1:T(8,128)(2,1)S(1)}, u32[]{:S(2)}, u32[]{:S(2)}) collective-permute-start(bf16[512,416]{0,1:T(8,128)(2,1)S(1)} %fusion.101), channel_id=1, source_target_pairs={{0,96},{32,0},{64,32},{96,64},{1,97},{33,1},{65,33},{97,65},{2,98}... | collective-permute-start | bytes 1277960 | tf_op jit(solution)/shard_map/ppermute | solution.py:94
  263.2 8.3 %collective-permute-start.15 = (bf16[512,416]{0,1:T(8,128)(2,1)S(1)}, bf16[512,416]{0,1:T(8,128)(2,1)S(1)}, u32[]{:S(2)}, u32[]{:S(2)}) collective-permute-start(bf16[512,416]{0,1:T(8,128)(2,1)S(1)} %add_convert_fusion.3), channel_id=1, source_target_pairs={{0,32},{32,64},{64,96},{96,0},{1,33},{33,65},{65,97},{97,1},{2,34}... | collective-permute-start | bytes 1277960 | tf_op jit(solution)/shard_map/ppermute | solution.py:93
  265.0 8.6 %collective-permute-start.18 = (bf16[512,416]{0,1:T(8,128)(2,1)S(1)}, bf16[512,416]{0,1:T(8,128)(2,1)S(1)}, u32[]{:S(2)}, u32[]{:S(2)}) collective-permute-start(bf16[512,416]{0,1:T(8,128)(2,1)S(1)} %add_convert_fusion.1), channel_id=1, source_target_pairs={{0,96},{32,0},{64,32},{96,64},{1,97},{33,1},{65,33},{97,65},{2,98}... | collective-permute-start | bytes 1277960 | tf_op jit(solution)/shard_map/ppermute | solution.py:94
  271.7 10.6 %collective-permute-start.16 = (bf16[512,416]{0,1:T(8,128)(2,1)S(1)}, bf16[512,416]{0,1:T(8,128)(2,1)S(1)}, u32[]{:S(2)}, u32[]{:S(2)}) collective-permute-start(bf16[512,416]{0,1:T(8,128)(2,1)S(1)} %add_convert_fusion.2), channel_id=1, source_target_pairs={{0,32},{32,64},{64,96},{96,0},{1,33},{33,65},{65,97},{97,1},{2,34}... | collective-permute-start | bytes 1277960 | tf_op jit(solution)/shard_map/ppermute | solution.py:93
  273.8 10.7 %collective-permute-start.19 = (bf16[512,416]{0,1:T(8,128)(2,1)S(1)}, bf16[512,416]{0,1:T(8,128)(2,1)S(1)}, u32[]{:S(2)}, u32[]{:S(2)}) collective-permute-start(bf16[512,416]{0,1:T(8,128)(2,1)S(1)} %add_convert_fusion), channel_id=1, source_target_pairs={{0,96},{32,0},{64,32},{96,64},{1,97},{33,1},{65,33},{97,65},{2,98}... | collective-permute-start | bytes 1277960 | tf_op jit(solution)/shard_map/ppermute | solution.py:94
  285.0 4.6 %collective-permute-start.20 = (f32[2,1024]{1,0:T(2,128)S(1)}, f32[2,1024]{1,0:T(2,128)S(1)}, u32[]{:S(2)}, u32[]{:S(2)}) collective-permute-start(f32[2,1024]{1,0:T(2,128)S(1)} %pad_maximum_fusion.2), channel_id=1, source_target_pairs={{0,96},{32,0},{64,32},{96,64},{1,97},{33,1},{65,33},{97,65},{2,98}... | collective-permute-start | bytes 24584 | tf_op jit(solution)/shard_map/ppermute | solution.py:110
  288.2 4.1 %collective-permute-start.21 = (f32[2,1024]{1,0:T(2,128)S(1)}, f32[2,1024]{1,0:T(2,128)S(1)}, u32[]{:S(2)}, u32[]{:S(2)}) collective-permute-start(f32[2,1024]{1,0:T(2,128)S(1)} %pad_maximum_fusion.2), channel_id=1, source_target_pairs={{0,64},{32,96},{64,0},{96,32},{1,65},{33,97},{65,1},{97,33},{2,66}... | collective-permute-start | bytes 24584 | tf_op jit(solution)/shard_map/ppermute | solution.py:110
  288.8 3.7 %collective-permute-start.22 = (f32[2,1024]{1,0:T(2,128)S(1)}, f32[2,1024]{1,0:T(2,128)S(1)}, u32[]{:S(2)}, u32[]{:S(2)}) collective-permute-start(f32[2,1024]{1,0:T(2,128)S(1)} %pad_maximum_fusion.2), channel_id=1, source_target_pairs={{0,32},{32,64},{64,96},{96,0},{1,33},{33,65},{65,97},{97,1},{2,34}... | collective-permute-start | bytes 24584 | tf_op jit(solution)/shard_map/ppermute | solution.py:110
  300.1 4.8 %collective-permute-start.23 = (bf16[128,416]{0,1:T(8,128)(2,1)S(1)}, bf16[128,416]{0,1:T(8,128)(2,1)S(1)}, u32[]{:S(2)}, u32[]{:S(2)}) collective-permute-start(bf16[128,416]{0,1:T(8,128)(2,1)S(1)} %fusion.142), channel_id=1, source_target_pairs={{0,32},{32,64},{64,96},{96,0},{1,33},{33,65},{65,97},{97,1},{2,34}... | collective-permute-start | bytes 319496 | tf_op jit(solution)/shard_map/ppermute | solution.py:74
  300.5 4.5 %collective-permute-start.26 = (bf16[128,416]{0,1:T(8,128)(2,1)S(1)}, bf16[128,416]{0,1:T(8,128)(2,1)S(1)}, u32[]{:S(2)}, u32[]{:S(2)}) collective-permute-start(bf16[128,416]{0,1:T(8,128)(2,1)S(1)} %fusion.143), channel_id=1, source_target_pairs={{0,96},{32,0},{64,32},{96,64},{1,97},{33,1},{65,33},{97,65},{2,98}... | collective-permute-start | bytes 319496 | tf_op jit(solution)/shard_map/ppermute | solution.py:75
  305.0 4.8 %collective-permute-start.24 = (bf16[128,416]{0,1:T(8,128)(2,1)S(1)}, bf16[128,416]{0,1:T(8,128)(2,1)S(1)}, u32[]{:S(2)}, u32[]{:S(2)}) collective-permute-start(bf16[128,416]{0,1:T(8,128)(2,1)S(1)} %fusion.141), channel_id=1, source_target_pairs={{0,32},{32,64},{64,96},{96,0},{1,33},{33,65},{65,97},{97,1},{2,34}... | collective-permute-start | bytes 319496 | tf_op jit(solution)/shard_map/ppermute | solution.py:74
  305.1 4.8 %collective-permute-start.27 = (bf16[128,416]{0,1:T(8,128)(2,1)S(1)}, bf16[128,416]{0,1:T(8,128)(2,1)S(1)}, u32[]{:S(2)}, u32[]{:S(2)}) collective-permute-start(bf16[128,416]{0,1:T(8,128)(2,1)S(1)} %fusion.138), channel_id=1, source_target_pairs={{0,96},{32,0},{64,32},{96,64},{1,97},{33,1},{65,33},{97,65},{2,98}... | collective-permute-start | bytes 319496 | tf_op jit(solution)/shard_map/ppermute | solution.py:75
  309.8 6.0 %collective-permute-start.25 = (bf16[128,416]{0,1:T(8,128)(2,1)S(1)}, bf16[128,416]{0,1:T(8,128)(2,1)S(1)}, u32[]{:S(2)}, u32[]{:S(2)}) collective-permute-start(bf16[128,416]{0,1:T(8,128)(2,1)S(1)} %fusion.140), channel_id=1, source_target_pairs={{0,32},{32,64},{64,96},{96,0},{1,33},{33,65},{65,97},{97,1},{2,34}... | collective-permute-start | bytes 319496 | tf_op jit(solution)/shard_map/ppermute | solution.py:74
  310.0 5.9 %collective-permute-start.28 = (bf16[128,416]{0,1:T(8,128)(2,1)S(1)}, bf16[128,416]{0,1:T(8,128)(2,1)S(1)}, u32[]{:S(2)}, u32[]{:S(2)}) collective-permute-start(bf16[128,416]{0,1:T(8,128)(2,1)S(1)} %fusion.137), channel_id=1, source_target_pairs={{0,96},{32,0},{64,32},{96,64},{1,97},{33,1},{65,33},{97,65},{2,98}... | collective-permute-start | bytes 319496 | tf_op jit(solution)/shard_map/ppermute | solution.py:75
Sparse Core Ops, SparseCore 0:
  9.6 46.5 all-gather.12
  58.5 49.1 all-gather.8
  109.9 49.4 all-gather.14
  161.5 49.7 all-gather.16
  213.4 48.9 all-gather.10

commit v3 on v2

--- a/solution.py
+++ b/solution.py
@@ -164,8 +164,10 @@
     feature_cols = tokens.shape[1]
     n_gx = lax.axis_size("gx")
     features = feature_cols * n_gx
-    qkv_all = lax.all_gather(query_key_value, "gy", axis=1, tiled=True)
-    proj_all = lax.all_gather(project_out, "gy", axis=1, tiled=True)
+    planes = jnp.concatenate([query_key_value, project_out.T[None]], axis=0)
+    planes_all = lax.all_gather(planes, "gy", axis=1, tiled=True)
+    qkv_all = planes_all[: query_key_value.shape[0]]
+    proj_all = planes_all[query_key_value.shape[0]].T
     up_all = lax.all_gather(up_weight, "gy", axis=0, tiled=True)
     down_all = lax.all_gather(down_weight, "gy", axis=1, tiled=True)
     merge_all = lax.all_gather(merge_weight, "gy", axis=2, tiled=True)

time: 356 us -> 341 us (0.958)
  waiting for transfers between devices: 149 us -> 98.6 us
  local copies, waits for them, and re-layouts: 28.8 us -> 55.7 us
  matrix products: 74.7 us -> 85.1 us
    all_gather x2 -> x1, waiting for transfers between devices: 55.9 us -> 13.1 us  [body(): planes_all = lax.all_gather(planes, 'gy', axis=1, tiled=True)]
    sub x1, matrix products: 11.4 us -> 23.8 us  [one_block(): raised = jnp.exp(scores - highest)]
    another operation x1 -> x2, local copies, waits for them, and re-layouts: 0.01 us -> 7.09 us
    ppermute x2, waiting for transfers between devices: 12.1 us -> 5.05 us  [gx_all_gather(): far_top = lax.ppermute(from_left[:half], 'gx', ring_perm(n, 1))]
    slice x1 -> x2, local copies, waits for them, and re-layouts: 0.18 us -> 6.65 us  [the longest x1 6.47 us: body(): proj_all = planes_all[query_key_value.shape[0]].T]
    reshape x0 -> x1, local copies, waits for them, and re-layouts: none -> 5.11 us  [body(): proj_all.reshape(proj_all.shape[0], n_gx, width).transpose(1, 0, 2)]
    unnamed x36 -> x44, local copies, waits for them, and re-layouts: 23.4 us -> 26.6 us
  transfers between devices with their start and end apart: 34 -> 33, of which waited for: 20 -> 19; matrix products, arithmetic and copies ran while one was open for 31% -> 42% of each run, Pallas kernels for 0% -> 0%
where the time goes in v3:
time: 341 us; the launch traced here: 338 us
  waiting for transfers between devices  98.6 us (29%)
  matrix products  85.1 us (25%)
  local copies, waits for them, and re-layouts  55.7 us (16%)
  starting transfers between devices  44.2 us (13%)
  blocking collectives  28.9 us (8%)
  between operations  14.5 us (4%)
  other arithmetic  10.9 us (3%)
    ppermute x2, waiting for transfers between devices, gx_all_gather(): from_left = lax.ppermute(x, 'gx', ring_perm(n, 1))  32.9 us
    ppermute x6, waiting for transfers between devices, gx_matmul_reduce_scatter(): got_top = lax.ppermute(acc_top.astype(jnp.bfloat16), 'gx', ring_perm(n, 1))  31.6 us
    all_to_all x1, blocking collectives, body(): lax.all_to_all(outgoing, 'gy', split_axis=0, concat_axis=0, tiled=True)  28.9 us
    unnamed x44, local copies, waits for them, and re-layouts  26.6 us
    dot_general x1, matrix products, body(): upper = jnp.dot(columns, up_all, preferred_element_type=jnp.float32)  26.2 us
    sub x1, matrix products, one_block(): raised = jnp.exp(scores - highest)  23.8 us
    ppermute x6, starting transfers between devices, gx_matmul_reduce_scatter(): lax.ppermute(acc_bottom.astype(jnp.bfloat16), 'gx', ring_perm(n, -1))  16.2 us
    all_gather x1, waiting for transfers between devices, body(): planes_all = lax.all_gather(planes, 'gy', axis=1, tiled=True)  13.1 us
  transfers between devices with their start and end apart: 33, of which 19 were waited for; matrix products, arithmetic and copies ran while one was open for 42% of the time, Pallas kernels for 0%

profile of v3, /device:TPU:1, one launch (start us, length us, event | category | flops | bytes accessed | tf_op | source)
XLA Modules:
  0.0 337.9 jit_solution(4849284636285559681)
XLA Ops:
  6.5 1.1 copy.56
  7.6 0.9 copy.57
  8.6 0.9 pad_maximum_fusion.2
  11.0 2.5 collective-permute-start.1
  13.6 2.2 collective-permute-start
  15.8 18.8 %collective-permute-done.1 = bf16[1024,416]{0,1:T(8,128)(2,1)S(1)} collective-permute-done((bf16[1024,416]{0,1:T(8,128)(2,1)}, bf16[1024,416]{0,1:T(8,128)(2,1)S(1)}, u32[]{:S(2)}, u32[]{:S(2)}) %collective-permute-start.1) | collective-permute-done | bytes 852000 | tf_op jit(solution)/shard_map/ppermute | solution.py:43
  34.7 0.8 slice.113
  35.5 3.0 collective-permute-start.3
  38.5 2.5 broadcast_compare_fusion
  40.9 5.0 %collective-permute-done.2 = bf16[512,416]{0,1:T(8,128)(2,1)S(1)} collective-permute-done((bf16[512,416]{0,1:T(8,128)(2,1)S(1)}, bf16[512,416]{0,1:T(8,128)(2,1)S(1)}, u32[]{:S(2)}, u32[]{:S(2)}) %collective-permute-start.2) | collective-permute-done | bytes 426016 | tf_op jit(solution)/shard_map/ppermute | solution.py:45
  46.4 1.0 constant_dynamic-update-slice_fusion
  48.8 1.0 fusion.24
  49.9 13.1 %all-gather.7.cloned.1.call-done = bf16[4,1664,416]{2,0,1:T(4,128)(2,1)} async-done(((bf16[4,52,416]{2,0,1:T(4,128)(2,1)}), bf16[4,1664,416]{2,0,1:T(4,128)(2,1)}) %all-gather.7.cloned.1.call-update) | async-done | bytes 5537808 | tf_op jit(solution)/shard_map/all_gather | solution.py:168
  63.0 6.5 %slice.118 = bf16[1,1664,416]{2,0,1:T(2,128)(2,1)S(1)} slice(bf16[4,1664,416]{2,0,1:T(4,128)(2,1)} %all-gather.7.cloned.1.call-done), slice={[3:4], [0:1664], [0:416]} | slice | bytes 2768896 | tf_op jit(solution)/shard_map/slice | solution.py:170
  69.5 7.1 %copy.81 = bf16[1,1664,416]{1,2,0:T(8,128)(2,1)} copy(bf16[1,1664,416]{2,0,1:T(2,128)(2,1)S(1)} %slice.118) | data formatting | bytes 2768896
  76.5 5.1 %reshape.186 = bf16[416,4,416]{2,1,0:T(4,128)(2,1)S(1)} reshape(bf16[416,1664]{1,0:T(8,128)(2,1)} %bitcast.184) | data formatting | bytes 2768896 | tf_op jit(solution)/shard_map/reshape | solution.py:175
  81.7 9.9 %convert_bitcast_fusion = bf16[3,1024,416]{1,2,0:T(8,128)(2,1)S(1)} fusion(f32[1664]{0:T(1024)S(1)} %copy-done.8, f32[1664]{0:T(1024)S(1)} %copy-done.9, f32[1024]{0:T(1024)S(1)} %add_rsqrt_fusion.2, f32[1024]{0:T(1024)S(1)} %broadcast_multiply_fusion.1, bf16[3,1664,416]{2,0,1:T(4,128)(2,1)} %bitcast.204, bf16[1024,416]{0,1:T(8,128)(2,1)} %copy-done.2, ...), kind=kOutput, calls=%fused_computation.64 | convolution fusion | flops 4276453376 | bytes 10138624 | tf_op jit(solution)/shard_map/td,kdc->ktc/dot_general | solution.py:180
  91.6 1.6 fusion.167
  93.2 23.8 %fusion.170 = (f32[4,1024]{1,0:T(4,128)S(1)}, f32[4,1024,1024]{1,2,0:T(8,128)}) fusion(pred[1024,1024]{0,1:T(8,128)(4,1)S(1)} %copy-done.6, bf16[1024,4,104]{0,2,1:T(8,128)(2,1)} %bitcast.208, bf16[1024,4,104]{0,2,1:T(8,128)(2,1)} %bitcast.207), kind=kOutput, calls=%fused_computation.233 | convolution fusion | flops 889193472 | bytes 19546112 | tf_op jit(solution)/shard_map/while/body/eval_jaxpr/sub | solution.py:137
  117.0 7.4 %fusion.95 = bf16[1024,4,104]{0,2,1:T(8,128)(2,1)S(1)} fusion(bf16[1024,4,104]{0,2,1:T(8,128)(2,1)} %bitcast.206, f32[4,1024,1024]{1,2,0:T(8,128)} %get-tuple-element.52, f32[4,1024]{1,0:T(4,128)S(1)} %get-tuple-element.51), kind=kOutput, calls=%fused_computation.109 | convolution fusion | flops 881229824 | bytes 18497536 | tf_op jit(solution)/shard_map/while/body/eval_jaxpr/hqk,khe->qhe/dot_general | solution.py:139
  124.5 7.1 %constant_dynamic-slice_fusion.6 = (bf16[416,1,416]{2,1,0:T(2,128)(2,1)S(1)}, bf16[416,1,416]{2,1,0:T(2,128)(2,1)S(1)}, bf16[416,1,416]{2,1,0:T(2,128)(2,1)S(1)}...) fusion(bf16[416,4,416]{2,1,0:T(4,128)(2,1)S(1)} %reshape.186, ...), kind=kLoop, calls=%fused_computation.217 | loop fusion | bytes 5537824 | tf_op jit(solution)/shard_map/dynamic-slice.1
  132.0 1.4 collective-permute-start.4
  133.8 1.5 collective-permute-start.7
  136.1 8.2 %collective-permute-done.4 = bf16[512,416]{0,1:T(8,128)(2,1)S(1)} collective-permute-done((bf16[512,416]{0,1:T(8,128)(2,1)S(1)}, bf16[512,416]{0,1:T(8,128)(2,1)S(1)}, u32[]{:S(2)}, u32[]{:S(2)}) %collective-permute-start.4) | collective-permute-done | bytes 426016 | tf_op jit(solution)/shard_map/ppermute | solution.py:93
  145.4 2.7 collective-permute-start.8
  148.5 7.9 %collective-permute-done.5 = bf16[512,416]{0,1:T(8,128)(2,1)S(1)} collective-permute-done((bf16[512,416]{0,1:T(8,128)(2,1)S(1)}, bf16[512,416]{0,1:T(8,128)(2,1)S(1)}, u32[]{:S(2)}, u32[]{:S(2)}) %collective-permute-start.5) | collective-permute-done | bytes 426016 | tf_op jit(solution)/shard_map/ppermute | solution.py:93
  156.8 2.7 collective-permute-start.9
  160.0 7.4 %collective-permute-done.6 = bf16[512,416]{0,1:T(8,128)(2,1)S(1)} collective-permute-done((bf16[512,416]{0,1:T(8,128)(2,1)S(1)}, bf16[512,416]{0,1:T(8,128)(2,1)S(1)}, u32[]{:S(2)}, u32[]{:S(2)}) %collective-permute-start.6) | collective-permute-done | bytes 426016 | tf_op jit(solution)/shard_map/ppermute | solution.py:93
  168.0 2.7 collective-permute-start.10
  172.8 14.1 %collective-permute-done.11 = bf16[1024,416]{0,1:T(8,128)(2,1)S(1)} collective-permute-done((bf16[1024,416]{0,1:T(8,128)(2,1)S(1)}, bf16[1024,416]{0,1:T(8,128)(2,1)S(1)}, u32[]{:S(2)}, u32[]{:S(2)}) %collective-permute-start.11) | collective-permute-done | bytes 852000 | tf_op jit(solution)/shard_map/ppermute | solution.py:43
  187.3 0.8 slice.121
  188.1 2.7 collective-permute-start.13
  190.9 8.6 %reshape.193 = bf16[1664,2048]{1,0:T(8,128)(2,1)} reshape(bf16[32,52,2048]{2,1,0:T(8,128)(2,1)} %all-gather.11.cloned.1.call-done) | data formatting | bytes 13631488
  199.5 8.6 %reshape.195 = bf16[1664,2048]{1,0:T(8,128)(2,1)} reshape(bf16[32,52,2048]{2,1,0:T(8,128)(2,1)} %all-gather.13.cloned.1.call-done) | data formatting | bytes 13631488
  208.1 1.3 constant_dynamic-update-slice_fusion.2
  210.5 1.4 fusion.20
  212.0 26.2 %fusion.4 = bf16[1024,2048]{1,0:T(8,128)(2,1)S(1)} fusion(bf16[1664,2048]{1,0:T(8,128)(2,1)S(1)} %bitcast.183, f32[1664]{0:T(1024)S(1)} %copy-done.10, f32[1664]{0:T(1024)S(1)} %copy-done.11, f32[1024]{0:T(1024)S(1)} %add_rsqrt_fusion.1, f32[1024]{0:T(1024)S(1)} %broadcast_multiply_fusion, bf16[1024,416]{0,1:T(8,128)(2,1)S(1)} %get-tuple-element.26, ...), kind=kOutput, calls=%fused_computation.12 | convolution fusion | flops 7137787904 | bytes 14439424 | tf_op jit(solution)/shard_map/dot_general | solution.py:192
  238.2 1.1 fusion.96
  239.3 1.1 fusion.101
  240.4 1.1 fusion.72
  241.5 2.7 collective-permute-start.17
  244.2 1.1 fusion.70
  245.3 2.2 collective-permute-done.14
  247.5 1.1 add_convert_fusion.3
  249.3 1.1 add_convert_fusion.1
  250.4 3.2 collective-permute-start.18
  253.6 1.1 fusion.64
  254.7 2.2 collective-permute-done.15
  257.1 1.7 collective-permute-done.18
  258.9 3.4 %collective-permute-start.19 = (bf16[512,416]{0,1:T(8,128)(2,1)S(1)}, bf16[512,416]{0,1:T(8,128)(2,1)S(1)}, u32[]{:S(2)}, u32[]{:S(2)}) collective-permute-start(bf16[512,416]{0,1:T(8,128)(2,1)S(1)} %add_convert_fusion), channel_id=1, source_target_pairs={{0,96},{32,0},{64,32},{96,64},{1,97},{33,1},{65,33},{97,65},{2,98}... | collective-permute-start | bytes 1277960 | tf_op jit(solution)/shard_map/ppermute | solution.py:94
  262.4 1.1 fusion.62
  263.4 3.8 %collective-permute-done.16 = bf16[512,416]{0,1:T(8,128)(2,1)S(1)} collective-permute-done((bf16[512,416]{0,1:T(8,128)(2,1)S(1)}, bf16[512,416]{0,1:T(8,128)(2,1)S(1)}, u32[]{:S(2)}, u32[]{:S(2)}) %collective-permute-start.16) | collective-permute-done | bytes 426016 | tf_op jit(solution)/shard_map/ppermute | solution.py:93
  267.3 2.1 collective-permute-done.19
  270.0 3.2 collective-permute-start.20
  273.9 3.3 collective-permute-done.21
  279.0 5.5 %fusion.46 = f32[256,1664]{1,0:T(8,128)S(1)} fusion(bf16[256,4,416]{2,0,1:T(8,128)(2,1)S(1)} %bitcast.205, bf16[4,416,1664]{1,0,2:T(4,128)(2,1)} %all-gather.9.cloned.1.call-done), kind=kOutput, calls=%fused_computation.60 | convolution fusion | flops 1417674752 | bytes 8093696 | tf_op jit(solution)/shard_map/pkf,kfc->pc/dot_general | solution.py:105
  285.3 2.7 collective-permute-start.26
  288.0 1.7 collective-permute-done.23
  289.9 3.0 collective-permute-start.27
  292.9 1.7 collective-permute-done.24
  294.7 3.0 collective-permute-start.28
  297.8 2.9 collective-permute-done.25
  301.3 28.9 %all_to_all.5 = bf16[32,16,416]{2,1,0:T(8,128)(2,1)S(1)} all-to-all(bf16[32,16,416]{2,1,0:T(8,128)(2,1)S(1)} %bitcast.202), channel_id=1, replica_groups=mesh['gx'=4,'gy'=32] {'gy'}, dimensions={0} | all-to-all | bytes 851968 | tf_op jit(solution)/shard_map/all_to_all | solution.py:230
  330.2 0.8 copy.135
  (141 shorter events, 17.7 us)
Async XLA Ops:
  6.5 41.0 %copy-start.4 = (bf16[1024,416]{0,1:T(8,128)(2,1)S(1)}, bf16[1024,416]{0,1:T(8,128)(2,1)}, u32[]{:S(2)}) copy-start(bf16[1024,416]{0,1:T(8,128)(2,1)} %param.14) | copy-start | bytes 2555908
  6.5 56.4 %all-gather.7.cloned.1.call-start = ((), (), s32[]{:S(2)}) async-start(), calls=%async_computation.1 | async-start | bytes 7028736 | tf_op jit(solution)/shard_map/all_gather | solution.py:168
  9.5 181.3 %all-gather.11.cloned.1.call-start = ((), (), s32[]{:S(2)}) async-start(), calls=%async_computation.3 | async-start | bytes 7569408 | tf_op jit(solution)/shard_map/all_gather | solution.py:171
  10.3 189.2 %all-gather.13.cloned.1.call-start = ((), (), s32[]{:S(2)}) async-start(), calls=%async_computation.4 | async-start | bytes 7569408 | tf_op jit(solution)/shard_map/all_gather | solution.py:172
  11.0 268.0 %all-gather.9.cloned.1.call-start = ((), (), s32[]{:S(2)}) async-start(), calls=%async_computation.2 | async-start | bytes 7028736 | tf_op jit(solution)/shard_map/all_gather | solution.py:173
  11.0 23.5 %collective-permute-start.1 = (bf16[1024,416]{0,1:T(8,128)(2,1)}, bf16[1024,416]{0,1:T(8,128)(2,1)S(1)}, u32[]{:S(2)}, u32[]{:S(2)}) collective-permute-start(bf16[1024,416]{0,1:T(8,128)(2,1)} %param.14), channel_id=1, source_target_pairs={{0,32},{32,64},{64,96},{96,0},{1,33},{33,65},{65,97},{97,1},{2,34}... | collective-permute-start | bytes 2555912 | tf_op jit(solution)/shard_map/ppermute | solution.py:43
  13.6 21.1 %collective-permute-start = (bf16[1024,416]{0,1:T(8,128)(2,1)}, bf16[1024,416]{0,1:T(8,128)(2,1)S(1)}, u32[]{:S(2)}, u32[]{:S(2)}) collective-permute-start(bf16[1024,416]{0,1:T(8,128)(2,1)} %param.14), channel_id=1, source_target_pairs={{0,96},{32,0},{64,32},{96,64},{1,97},{33,1},{65,33},{97,65},{2,98}... | collective-permute-start | bytes 2555912 | tf_op jit(solution)/shard_map/ppermute | solution.py:44
  34.6 11.4 %collective-permute-start.2 = (bf16[512,416]{0,1:T(8,128)(2,1)S(1)}, bf16[512,416]{0,1:T(8,128)(2,1)S(1)}, u32[]{:S(2)}, u32[]{:S(2)}) collective-permute-start(bf16[512,416]{0,1:T(8,128)(2,1)S(1)} %slice.112), channel_id=1, source_target_pairs={{0,32},{32,64},{64,96},{96,0},{1,33},{33,65},{65,97},{97,1},{2,34}... | collective-permute-start | bytes 1277960 | tf_op jit(solution)/shard_map/ppermute | solution.py:45
  35.5 11.0 %collective-permute-start.3 = (bf16[512,416]{0,1:T(8,128)(2,1)}, bf16[512,416]{0,1:T(8,128)(2,1)}, u32[]{:S(2)}, u32[]{:S(2)}) collective-permute-start(bf16[512,416]{0,1:T(8,128)(2,1)} %slice.113), channel_id=1, source_target_pairs={{0,96},{32,0},{64,32},{96,64},{1,97},{33,1},{65,33},{97,65},{2,98}... | collective-permute-start | bytes 1277960 | tf_op jit(solution)/shard_map/ppermute | solution.py:46
  47.9 0.9 copy-start
  47.9 2.0 copy-start.1
  47.9 1.9 copy-start.2
  47.9 1.9 copy-start.3
  49.9 31.7 %copy-start.8 = (f32[1664]{0:T(1024)S(1)}, f32[1664]{0:T(1024)}, u32[]{:S(2)}) copy-start(f32[1664]{0:T(1024)} %param.17) | copy-start | bytes 19972
  49.9 31.7 %copy-start.9 = (f32[1664]{0:T(1024)S(1)}, f32[1664]{0:T(1024)}, u32[]{:S(2)}) copy-start(f32[1664]{0:T(1024)} %param.16) | copy-start | bytes 19972
  81.7 11.5 %copy-start.6 = (pred[1024,1024]{0,1:T(8,128)(4,1)S(1)}, pred[1024,1024]{0,1:T(8,128)(4,1)}, u32[]{:S(2)}) copy-start(pred[1024,1024]{0,1:T(8,128)(4,1)} %broadcast_compare_fusion) | copy-start | bytes 3145732
  132.0 12.4 %collective-permute-start.4 = (bf16[512,416]{0,1:T(8,128)(2,1)S(1)}, bf16[512,416]{0,1:T(8,128)(2,1)S(1)}, u32[]{:S(2)}, u32[]{:S(2)}) collective-permute-start(bf16[512,416]{0,1:T(8,128)(2,1)S(1)} %convolution_convert_fusion.2), channel_id=1, source_target_pairs={{0,32},{32,64},{64,96},{96,0},{1,33},{33,65},{65,97},{97,1},{2,34}... | collective-permute-start | bytes 1277960 | tf_op jit(solution)/shard_map/ppermute | solution.py:93
  133.8 11.2 %collective-permute-start.7 = (bf16[512,416]{0,1:T(8,128)(2,1)S(1)}, bf16[512,416]{0,1:T(8,128)(2,1)S(1)}, u32[]{:S(2)}, u32[]{:S(2)}) collective-permute-start(bf16[512,416]{0,1:T(8,128)(2,1)S(1)} %convolution_convert_fusion.1), channel_id=1, source_target_pairs={{0,96},{32,0},{64,32},{96,64},{1,97},{33,1},{65,33},{97,65},{2,98}... | collective-permute-start | bytes 1277960 | tf_op jit(solution)/shard_map/ppermute | solution.py:94
  144.8 22.8 %copy-start.5 = (bf16[1024,416]{0,1:T(8,128)(2,1)S(1)}, bf16[1024,416]{0,1:T(8,128)(2,1)}, u32[]{:S(2)}) copy-start(bf16[1024,416]{0,1:T(8,128)(2,1)} %param.14) | copy-start | bytes 2555908
  144.8 11.6 %collective-permute-start.5 = (bf16[512,416]{0,1:T(8,128)(2,1)S(1)}, bf16[512,416]{0,1:T(8,128)(2,1)S(1)}, u32[]{:S(2)}, u32[]{:S(2)}) collective-permute-start(bf16[512,416]{0,1:T(8,128)(2,1)S(1)} %add_convert_fusion.7), channel_id=1, source_target_pairs={{0,32},{32,64},{64,96},{96,0},{1,33},{33,65},{65,97},{97,1},{2,34}... | collective-permute-start | bytes 1277960 | tf_op jit(solution)/shard_map/ppermute | solution.py:93
  145.4 11.2 %collective-permute-start.8 = (bf16[512,416]{0,1:T(8,128)(2,1)S(1)}, bf16[512,416]{0,1:T(8,128)(2,1)S(1)}, u32[]{:S(2)}, u32[]{:S(2)}) collective-permute-start(bf16[512,416]{0,1:T(8,128)(2,1)S(1)} %add_convert_fusion.5), channel_id=1, source_target_pairs={{0,96},{32,0},{64,32},{96,64},{1,97},{33,1},{65,33},{97,65},{2,98}... | collective-permute-start | bytes 1277960 | tf_op jit(solution)/shard_map/ppermute | solution.py:94
  148.5 23.7 %copy-start.7 = (s32[256,1]{0,1:T(1,128)S(1)}, s32[256,1]{0,1:T(1,128)}, u32[]{:S(2)}) copy-start(s32[256,1]{0,1:T(1,128)} %param.27) | copy-start | bytes 3076
  156.6 10.8 %collective-permute-start.6 = (bf16[512,416]{0,1:T(8,128)(2,1)S(1)}, bf16[512,416]{0,1:T(8,128)(2,1)S(1)}, u32[]{:S(2)}, u32[]{:S(2)}) collective-permute-start(bf16[512,416]{0,1:T(8,128)(2,1)S(1)} %add_convert_fusion.6), channel_id=1, source_target_pairs={{0,32},{32,64},{64,96},{96,0},{1,33},{33,65},{65,97},{97,1},{2,34}... | collective-permute-start | bytes 1277960 | tf_op jit(solution)/shard_map/ppermute | solution.py:93
  156.8 10.7 %collective-permute-start.9 = (bf16[512,416]{0,1:T(8,128)(2,1)S(1)}, bf16[512,416]{0,1:T(8,128)(2,1)S(1)}, u32[]{:S(2)}, u32[]{:S(2)}) collective-permute-start(bf16[512,416]{0,1:T(8,128)(2,1)S(1)} %add_convert_fusion.4), channel_id=1, source_target_pairs={{0,96},{32,0},{64,32},{96,64},{1,97},{33,1},{65,33},{97,65},{2,98}... | collective-permute-start | bytes 1277960 | tf_op jit(solution)/shard_map/ppermute | solution.py:94
  167.9 19.0 %collective-permute-start.11 = (bf16[1024,416]{0,1:T(8,128)(2,1)S(1)}, bf16[1024,416]{0,1:T(8,128)(2,1)S(1)}, u32[]{:S(2)}, u32[]{:S(2)}) collective-permute-start(bf16[1024,416]{0,1:T(8,128)(2,1)S(1)} %fusion.60), channel_id=1, source_target_pairs={{0,32},{32,64},{64,96},{96,0},{1,33},{33,65},{65,97},{97,1},{2,34}... | collective-permute-start | bytes 2555912 | tf_op jit(solution)/shard_map/ppermute | solution.py:43
  168.0 19.3 %collective-permute-start.10 = (bf16[1024,416]{0,1:T(8,128)(2,1)S(1)}, bf16[1024,416]{0,1:T(8,128)(2,1)S(1)}, u32[]{:S(2)}, u32[]{:S(2)}) collective-permute-start(bf16[1024,416]{0,1:T(8,128)(2,1)S(1)} %fusion.60), channel_id=1, source_target_pairs={{0,96},{32,0},{64,32},{96,64},{1,97},{33,1},{65,33},{97,65},{2,98}... | collective-permute-start | bytes 2555912 | tf_op jit(solution)/shard_map/ppermute | solution.py:44
  187.0 21.1 %collective-permute-start.12 = (bf16[512,416]{0,1:T(8,128)(2,1)S(1)}, bf16[512,416]{0,1:T(8,128)(2,1)S(1)}, u32[]{:S(2)}, u32[]{:S(2)}) collective-permute-start(bf16[512,416]{0,1:T(8,128)(2,1)S(1)} %slice.120), channel_id=1, source_target_pairs={{0,32},{32,64},{64,96},{96,0},{1,33},{33,65},{65,97},{97,1},{2,34}... | collective-permute-start | bytes 1277960 | tf_op jit(solution)/shard_map/ppermute | solution.py:45
  188.1 20.0 %collective-permute-start.13 = (bf16[512,416]{0,1:T(8,128)(2,1)}, bf16[512,416]{0,1:T(8,128)(2,1)}, u32[]{:S(2)}, u32[]{:S(2)}) collective-permute-start(bf16[512,416]{0,1:T(8,128)(2,1)} %slice.121), channel_id=1, source_target_pairs={{0,96},{32,0},{64,32},{96,64},{1,97},{33,1},{65,33},{97,65},{2,98}... | collective-permute-start | bytes 1277960 | tf_op jit(solution)/shard_map/ppermute | solution.py:46
  208.1 3.8 %slice-start.2 = ((s8[6815744]{0:T(1024)(128)(4,1)}), s8[4194304]{0:T(1024)(128)(4,1)S(1)}, s32[]{:S(2)}) async-start(s8[6815744]{0:T(1024)(128)(4,1)} %bitcast.182), calls=%async_computation.7 | async-start | bytes 8388608
  209.4 2.5 slice-start.3
  209.4 2.5 copy-start.10
  209.4 2.5 copy-start.11
  210.5 27.7 %slice-start = ((s8[6815744]{0:T(1024)(128)(4,1)}), s8[4194304]{0:T(1024)(128)(4,1)S(1)}, s32[]{:S(2)}) async-start(s8[6815744]{0:T(1024)(128)(4,1)} %bitcast.172), calls=%async_computation.5 | async-start | bytes 8388608
  212.0 26.2 %slice-start.1 = ((s8[6815744]{0:T(1024)(128)(4,1)}), s8[2621440]{0:T(1024)(128)(4,1)S(1)}, s32[]{:S(2)}) async-start(s8[6815744]{0:T(1024)(128)(4,1)} %bitcast.172), calls=%async_computation.6 | async-start | bytes 5242880
  239.3 8.3 %collective-permute-start.14 = (bf16[512,416]{0,1:T(8,128)(2,1)S(1)}, bf16[512,416]{0,1:T(8,128)(2,1)S(1)}, u32[]{:S(2)}, u32[]{:S(2)}) collective-permute-start(bf16[512,416]{0,1:T(8,128)(2,1)S(1)} %fusion.96), channel_id=1, source_target_pairs={{0,32},{32,64},{64,96},{96,0},{1,33},{33,65},{65,97},{97,1},{2,34}... | collective-permute-start | bytes 1277960 | tf_op jit(solution)/shard_map/ppermute | solution.py:93
  241.5 7.8 %collective-permute-start.17 = (bf16[512,416]{0,1:T(8,128)(2,1)S(1)}, bf16[512,416]{0,1:T(8,128)(2,1)S(1)}, u32[]{:S(2)}, u32[]{:S(2)}) collective-permute-start(bf16[512,416]{0,1:T(8,128)(2,1)S(1)} %fusion.101), channel_id=1, source_target_pairs={{0,96},{32,0},{64,32},{96,64},{1,97},{33,1},{65,33},{97,65},{2,98}... | collective-permute-start | bytes 1277960 | tf_op jit(solution)/shard_map/ppermute | solution.py:94
  248.6 8.3 %collective-permute-start.15 = (bf16[512,416]{0,1:T(8,128)(2,1)S(1)}, bf16[512,416]{0,1:T(8,128)(2,1)S(1)}, u32[]{:S(2)}, u32[]{:S(2)}) collective-permute-start(bf16[512,416]{0,1:T(8,128)(2,1)S(1)} %add_convert_fusion.3), channel_id=1, source_target_pairs={{0,32},{32,64},{64,96},{96,0},{1,33},{33,65},{65,97},{97,1},{2,34}... | collective-permute-start | bytes 1277960 | tf_op jit(solution)/shard_map/ppermute | solution.py:93
  250.4 8.4 %collective-permute-start.18 = (bf16[512,416]{0,1:T(8,128)(2,1)S(1)}, bf16[512,416]{0,1:T(8,128)(2,1)S(1)}, u32[]{:S(2)}, u32[]{:S(2)}) collective-permute-start(bf16[512,416]{0,1:T(8,128)(2,1)S(1)} %add_convert_fusion.1), channel_id=1, source_target_pairs={{0,96},{32,0},{64,32},{96,64},{1,97},{33,1},{65,33},{97,65},{2,98}... | collective-permute-start | bytes 1277960 | tf_op jit(solution)/shard_map/ppermute | solution.py:94
  257.0 10.2 %collective-permute-start.16 = (bf16[512,416]{0,1:T(8,128)(2,1)S(1)}, bf16[512,416]{0,1:T(8,128)(2,1)S(1)}, u32[]{:S(2)}, u32[]{:S(2)}) collective-permute-start(bf16[512,416]{0,1:T(8,128)(2,1)S(1)} %add_convert_fusion.2), channel_id=1, source_target_pairs={{0,32},{32,64},{64,96},{96,0},{1,33},{33,65},{65,97},{97,1},{2,34}... | collective-permute-start | bytes 1277960 | tf_op jit(solution)/shard_map/ppermute | solution.py:93
  258.9 10.5 %collective-permute-start.19 = (bf16[512,416]{0,1:T(8,128)(2,1)S(1)}, bf16[512,416]{0,1:T(8,128)(2,1)S(1)}, u32[]{:S(2)}, u32[]{:S(2)}) collective-permute-start(bf16[512,416]{0,1:T(8,128)(2,1)S(1)} %add_convert_fusion), channel_id=1, source_target_pairs={{0,96},{32,0},{64,32},{96,64},{1,97},{33,1},{65,33},{97,65},{2,98}... | collective-permute-start | bytes 1277960 | tf_op jit(solution)/shard_map/ppermute | solution.py:94
  270.0 4.0 %collective-permute-start.20 = (f32[2,1024]{1,0:T(2,128)S(1)}, f32[2,1024]{1,0:T(2,128)S(1)}, u32[]{:S(2)}, u32[]{:S(2)}) collective-permute-start(f32[2,1024]{1,0:T(2,128)S(1)} %pad_maximum_fusion.3), channel_id=1, source_target_pairs={{0,96},{32,0},{64,32},{96,64},{1,97},{33,1},{65,33},{97,65},{2,98}... | collective-permute-start | bytes 24584 | tf_op jit(solution)/shard_map/ppermute | solution.py:110
  273.2 4.1 %collective-permute-start.21 = (f32[2,1024]{1,0:T(2,128)S(1)}, f32[2,1024]{1,0:T(2,128)S(1)}, u32[]{:S(2)}, u32[]{:S(2)}) collective-permute-start(f32[2,1024]{1,0:T(2,128)S(1)} %pad_maximum_fusion.3), channel_id=1, source_target_pairs={{0,64},{32,96},{64,0},{96,32},{1,65},{33,97},{65,1},{97,33},{2,66}... | collective-permute-start | bytes 24584 | tf_op jit(solution)/shard_map/ppermute | solution.py:110
  273.3 4.0 %collective-permute-start.22 = (f32[2,1024]{1,0:T(2,128)S(1)}, f32[2,1024]{1,0:T(2,128)S(1)}, u32[]{:S(2)}, u32[]{:S(2)}) collective-permute-start(f32[2,1024]{1,0:T(2,128)S(1)} %pad_maximum_fusion.3), channel_id=1, source_target_pairs={{0,32},{32,64},{64,96},{96,0},{1,33},{33,65},{65,97},{97,1},{2,34}... | collective-permute-start | bytes 24584 | tf_op jit(solution)/shard_map/ppermute | solution.py:110
  284.9 4.8 %collective-permute-start.23 = (bf16[128,416]{0,1:T(8,128)(2,1)S(1)}, bf16[128,416]{0,1:T(8,128)(2,1)S(1)}, u32[]{:S(2)}, u32[]{:S(2)}) collective-permute-start(bf16[128,416]{0,1:T(8,128)(2,1)S(1)} %fusion.142), channel_id=1, source_target_pairs={{0,32},{32,64},{64,96},{96,0},{1,33},{33,65},{65,97},{97,1},{2,34}... | collective-permute-start | bytes 319496 | tf_op jit(solution)/shard_map/ppermute | solution.py:74
  285.3 4.5 %collective-permute-start.26 = (bf16[128,416]{0,1:T(8,128)(2,1)S(1)}, bf16[128,416]{0,1:T(8,128)(2,1)S(1)}, u32[]{:S(2)}, u32[]{:S(2)}) collective-permute-start(bf16[128,416]{0,1:T(8,128)(2,1)S(1)} %fusion.143), channel_id=1, source_target_pairs={{0,96},{32,0},{64,32},{96,64},{1,97},{33,1},{65,33},{97,65},{2,98}... | collective-permute-start | bytes 319496 | tf_op jit(solution)/shard_map/ppermute | solution.py:75
  289.7 4.8 %collective-permute-start.24 = (bf16[128,416]{0,1:T(8,128)(2,1)S(1)}, bf16[128,416]{0,1:T(8,128)(2,1)S(1)}, u32[]{:S(2)}, u32[]{:S(2)}) collective-permute-start(bf16[128,416]{0,1:T(8,128)(2,1)S(1)} %fusion.141), channel_id=1, source_target_pairs={{0,32},{32,64},{64,96},{96,0},{1,33},{33,65},{65,97},{97,1},{2,34}... | collective-permute-start | bytes 319496 | tf_op jit(solution)/shard_map/ppermute | solution.py:74
  289.9 4.8 %collective-permute-start.27 = (bf16[128,416]{0,1:T(8,128)(2,1)S(1)}, bf16[128,416]{0,1:T(8,128)(2,1)S(1)}, u32[]{:S(2)}, u32[]{:S(2)}) collective-permute-start(bf16[128,416]{0,1:T(8,128)(2,1)S(1)} %fusion.138), channel_id=1, source_target_pairs={{0,96},{32,0},{64,32},{96,64},{1,97},{33,1},{65,33},{97,65},{2,98}... | collective-permute-start | bytes 319496 | tf_op jit(solution)/shard_map/ppermute | solution.py:75
  294.6 6.0 %collective-permute-start.25 = (bf16[128,416]{0,1:T(8,128)(2,1)S(1)}, bf16[128,416]{0,1:T(8,128)(2,1)S(1)}, u32[]{:S(2)}, u32[]{:S(2)}) collective-permute-start(bf16[128,416]{0,1:T(8,128)(2,1)S(1)} %fusion.140), channel_id=1, source_target_pairs={{0,32},{32,64},{64,96},{96,0},{1,33},{33,65},{65,97},{97,1},{2,34}... | collective-permute-start | bytes 319496 | tf_op jit(solution)/shard_map/ppermute | solution.py:74
  294.7 5.9 %collective-permute-start.28 = (bf16[128,416]{0,1:T(8,128)(2,1)S(1)}, bf16[128,416]{0,1:T(8,128)(2,1)S(1)}, u32[]{:S(2)}, u32[]{:S(2)}) collective-permute-start(bf16[128,416]{0,1:T(8,128)(2,1)S(1)} %fusion.137), channel_id=1, source_target_pairs={{0,96},{32,0},{64,32},{96,64},{1,97},{33,1},{65,33},{97,65},{2,98}... | collective-permute-start | bytes 319496 | tf_op jit(solution)/shard_map/ppermute | solution.py:75
Sparse Core Ops, SparseCore 0:
  9.6 53.2 all-gather.6
  65.2 49.4 all-gather.10
  117.0 49.7 all-gather.12
  170.8 50.4 all-gather.8
